TPU v7x, 512 devices: a whole 4x8x8 slice. The times are simulated.
512 devices in a mesh: dp: 32 (over x, y), expert: 16 (over z, core).
Axes of the slice: x: 4, y: 8, z: 8, core: 2. Of those that a mesh axis runs over, the one named last changes fastest.
Arguments:
- tokens: bfloat16 [65536, 2048], P(('dp', 'expert')), may hold values from -6 to 6
- cotangent: bfloat16 [65536, 2048], P(('dp', 'expert')), may hold values from -6 to 6
- expert_ids: int32 [65536, 2], P(('dp', 'expert')), may hold values from 0 to 15, as said below
- router_probs: float32 [65536, 2], P(('dp', 'expert')), may hold values from 0.1 to 1
- gate_weight: bfloat16 [16, 2048, 768], P('expert', 'dp'), may hold values from -0.125 to 0.125
- up_weight: bfloat16 [16, 2048, 768], P('expert', 'dp'), may hold values from -0.125 to 0.125
- down_weight: bfloat16 [16, 768, 2048], P('expert', 'dp'), may hold values from -0.21875 to 0.21875
Outputs:
- mixed_out: bfloat16 [65536, 2048], P(('dp', 'expert'))
- grad_tokens: bfloat16 [65536, 2048], P(('dp', 'expert'))
- grad_probs: float32 [65536, 2], P(('dp', 'expert'))
- grad_down: bfloat16 [16, 768, 2048], P('expert', 'dp')
Inputs may be any that keep to these rules, and one draw needn't show every extreme that they name: `expert_ids`: each token names 2 different experts. In each aligned block of 128 tokens (the tokens of one device) no expert is named more than 18 times, and in each aligned group of 16 such blocks one expert is named exactly 18 times in every block of the group.
All inputs are finite; a program needn't handle non-finite values.
Results may differ from a plain program's by a relative error of at most 0.023.
Values may be sent and summed in bfloat16 or wider, within the bound.
No kernel may reach another device: no remote copies, remote signals or barrier semaphores. Data moves between devices by JAX's collectives and lax.ppermute only.
A program may use at most 64 MiB of HBM per device.

v0:
```python
import jax
import jax.numpy as jnp
from jax import lax
from jax.sharding import PartitionSpec as P


def shards(tokens, cotangent, expert_ids, router_probs, gate_weight, up_weight, down_weight):
    tok_count = tokens.shape[0]
    features = tokens.shape[1]
    choices_each = expert_ids.shape[1]
    slot_total = tok_count * choices_each
    groups = lax.axis_size("expert")
    capacity = 9 * slot_total // (8 * groups)
    slot_count = groups * capacity
    flat_ids = expert_ids.reshape(slot_total)
    member = (flat_ids[:, None] == jnp.arange(groups, dtype=jnp.int32)[None, :]).astype(jnp.int32)
    before = jnp.cumsum(member, axis=0) - member
    target = flat_ids * capacity + jnp.sum(before * member, axis=1)
    placer = (target[None, :] == jnp.arange(slot_count, dtype=jnp.int32)[:, None]).astype(
        jnp.bfloat16
    )
    placer_tok = jnp.sum(placer.reshape(slot_count, tok_count, choices_each), axis=2)
    weighted = (
        (router_probs[:, :, None] * cotangent.astype(jnp.float32)[:, None, :])
        .astype(jnp.bfloat16)
        .reshape(slot_total, features)
    )
    send_rows = jnp.dot(placer_tok, tokens, preferred_element_type=jnp.float32).astype(jnp.bfloat16)
    send_grad = jnp.dot(placer, weighted, preferred_element_type=jnp.float32).astype(jnp.bfloat16)
    recv_rows, recv_grad = (
        lax.all_to_all(
            send_rows.reshape(groups, capacity, features),
            "expert",
            split_axis=0,
            concat_axis=0,
            tiled=True,
        ),
        lax.all_to_all(
            send_grad.reshape(groups, capacity, features),
            "expert",
            split_axis=0,
            concat_axis=0,
            tiled=True,
        ),
    )
    x_rows = recv_rows.reshape(slot_count, features)
    dy_rows = recv_grad.reshape(slot_count, features)
    w_gate, w_up = (
        lax.all_gather(gate_weight[0], "dp", axis=0, tiled=True),
        lax.all_gather(up_weight[0], "dp", axis=0, tiled=True),
    )
    gate_pre = jnp.dot(x_rows, w_gate, preferred_element_type=jnp.float32)
    up_pre = jnp.dot(x_rows, w_up, preferred_element_type=jnp.float32)
    sig_gate = jax.nn.sigmoid(gate_pre)
    active = gate_pre * sig_gate
    hidden = (active * up_pre).astype(jnp.bfloat16)
    contract = (((1,), (1,)), ((), ()))
    weight_rows = lax.all_gather(down_weight[0], "dp", axis=0, tiled=True)
    part_hidden = hidden
    acc_part = jnp.dot(part_hidden, weight_rows, preferred_element_type=jnp.float32)
    back_part = lax.dot_general(dy_rows, weight_rows, contract, preferred_element_type=jnp.float32)
    output = acc_part.astype(jnp.bfloat16)
    grad_gate = (back_part * up_pre * sig_gate * (1.0 + gate_pre * (1.0 - sig_gate))).astype(
        jnp.bfloat16
    )
    grad_up = (back_part * active).astype(jnp.bfloat16)
    grad_rows = (
        lax.dot_general(grad_gate, w_gate, contract, preferred_element_type=jnp.float32)
        + lax.dot_general(grad_up, w_up, contract, preferred_element_type=jnp.float32)
    ).astype(jnp.bfloat16)
    back_out, back_grad = (
        lax.all_to_all(
            output.reshape(groups, capacity, features),
            "expert",
            split_axis=0,
            concat_axis=0,
            tiled=True,
        ),
        lax.all_to_all(
            grad_rows.reshape(groups, capacity, features),
            "expert",
            split_axis=0,
            concat_axis=0,
            tiled=True,
        ),
    )
    unplace = (((0,), (0,)), ((), ()))
    gathered = lax.dot_general(
        placer, back_out.reshape(slot_count, features), unplace, preferred_element_type=jnp.float32
    )
    gathered = gathered.reshape(tok_count, choices_each, features)
    grad_tokens = lax.dot_general(
        placer_tok,
        back_grad.reshape(slot_count, features),
        unplace,
        preferred_element_type=jnp.float32,
    ).astype(jnp.bfloat16)
    mixed_out = jnp.sum(router_probs[:, :, None] * gathered, axis=1).astype(jnp.bfloat16)
    grad_probs = jnp.sum(cotangent.astype(jnp.float32)[:, None, :] * gathered, axis=2)
    part_hidden = hidden
    grad_down = lax.psum_scatter(
        lax.dot_general(
            part_hidden, dy_rows, (((0,), (0,)), ((), ())), preferred_element_type=jnp.float32
        ).astype(jnp.bfloat16),
        "dp",
        scatter_dimension=0,
        tiled=True,
    )[None]
    return (mixed_out, grad_tokens, grad_probs, grad_down)


def solution(mesh):
    placed = (
        P(("dp", "expert"), None),
        P(("dp", "expert"), None),
        P(("dp", "expert"), None),
        P(("dp", "expert"), None),
        P("expert", "dp", None),
        P("expert", "dp", None),
        P("expert", "dp", None),
    )
    return jax.shard_map(
        shards,
        mesh=mesh,
        in_specs=placed,
        out_specs=(
            P(("dp", "expert"), None),
            P(("dp", "expert"), None),
            P(("dp", "expert"), None),
            P("expert", "dp", None),
        ),
        check_vma=False,
    )
```

profile of v0, /device:TPU:1, one launch (start us, length us, event | category | flops | bytes accessed | tf_op | source)
XLA Modules:
  0.0 501.9 jit_solution(4395308883108628984)
XLA Ops:
  12.8 1.3 reshape.96
  14.2 11.9 %all-to-all-start = ((bf16[16,18,2048]{2,1,0:T(8,128)(2,1)}), bf16[16,18,2048]{2,1,0:T(8,128)(2,1)}, u32[]{:S(2)}, u32[]{:S(2)}) async-start(bf16[16,18,2048]{2,1,0:T(8,128)(2,1)} %reshape.96), calls=%async_computation | async-start | bytes 3145728 | tf_op jit(solution)/shard_map/all_to_all | solution.py:31
  26.4 1.0 mul.83.clone
  27.4 2.5 mul.84
  29.9 2.2 convolution_convert_fusion.2
  32.1 1.4 reshape.100
  33.4 31.3 %all-to-all-done = bf16[16,18,2048]{2,1,0:T(8,128)(2,1)} async-done(((bf16[16,18,2048]{2,1,0:T(8,128)(2,1)}), bf16[16,18,2048]{2,1,0:T(8,128)(2,1)}, u32[]{:S(2)}, u32[]{:S(2)}) %all-to-all-start) | async-done | bytes 1179680 | tf_op jit(solution)/shard_map/all_to_all | solution.py:31
  64.7 4.1 all-to-all-start.2
  68.9 2.4 reshape.97
  71.3 36.1 %all-to-all-done.2 = bf16[16,18,2048]{2,1,0:T(8,128)(2,1)S(1)} async-done(((bf16[16,18,2048]{2,1,0:T(8,128)(2,1)}), bf16[16,18,2048]{2,1,0:T(8,128)(2,1)S(1)}, u32[]{:S(2)}, u32[]{:S(2)}) %all-to-all-start.2) | async-done | bytes 1179680 | tf_op jit(solution)/shard_map/all_to_all | solution.py:38
  107.4 1.2 reshape.101
  108.6 4.3 fusion.10
  113.0 69.5 %all-gather.9.cloned.1.call-done = bf16[1,2048,768]{2,1,0:T(8,128)(2,1)} async-done(((bf16[1,64,768]{2,1,0:T(8,128)(2,1)}), bf16[1,2048,768]{2,1,0:T(8,128)(2,1)}) %all-gather.9.cloned.1.call-update) | async-done | bytes 3145744 | tf_op jit(solution)/shard_map/all_gather | solution.py:50
  182.5 4.1 multiply_convert_fusion.4
  187.4 3.6 convolution_convert_fusion
  191.0 76.5 %all-gather.11.cloned.1.call-done = bf16[1,768,2048]{2,1,0:T(8,128)(2,1)} async-done(((bf16[1,24,2048]{2,1,0:T(8,128)(2,1)}), bf16[1,768,2048]{2,1,0:T(8,128)(2,1)}) %all-gather.11.cloned.1.call-update) | async-done | bytes 3145744 | tf_op jit(solution)/shard_map/all_gather | solution.py:58
  267.5 3.0 fusion.18
  270.5 1.4 reshape.98
  271.8 11.9 %all-to-all-start.1 = ((bf16[16,18,2048]{2,1,0:T(8,128)(2,1)}), bf16[16,18,2048]{2,1,0:T(8,128)(2,1)S(1)}, u32[]{:S(2)}, u32[]{:S(2)}) async-start(bf16[16,18,2048]{2,1,0:T(8,128)(2,1)} %reshape.98), calls=%async_computation.1 | async-start | bytes 3145728 | tf_op jit(solution)/shard_map/all_to_all | solution.py:72
  283.7 3.5 fusion
  287.3 1.1 fusion.4
  289.4 2.2 fusion.15
  291.7 2.4 reshape.102
  294.0 28.2 %all-to-all-done.1 = bf16[16,18,2048]{2,1,0:T(8,128)(2,1)S(1)} async-done(((bf16[16,18,2048]{2,1,0:T(8,128)(2,1)}), bf16[16,18,2048]{2,1,0:T(8,128)(2,1)S(1)}, u32[]{:S(2)}, u32[]{:S(2)}) %all-to-all-start.1) | async-done | bytes 1179680 | tf_op jit(solution)/shard_map/all_to_all | solution.py:72
  322.2 4.3 all-to-all-start.3
  326.5 1.1 convert_element_type.58
  327.6 1.2 reshape.107
  328.8 36.2 %all-to-all-done.3 = bf16[16,18,2048]{2,1,0:T(8,128)(2,1)} async-done(((bf16[16,18,2048]{2,1,0:T(8,128)(2,1)}), bf16[16,18,2048]{2,1,0:T(8,128)(2,1)}, u32[]{:S(2)}, u32[]{:S(2)}) %all-to-all-start.3) | async-done | bytes 1179680 | tf_op jit(solution)/shard_map/all_to_all | solution.py:79
  365.0 1.6 reshape.103
  366.6 3.0 multiply_reduce_fusion
  369.6 1.3 convolution_convert_fusion.3
  370.9 124.5 %reduce-scatter.2.cloned.1.call-done = bf16[24,2048]{1,0:T(8,128)(2,1)} async-done(((bf16[768,2048]{1,0:T(8,128)(2,1)}), bf16[24,2048]{1,0:T(8,128)(2,1)}) %reduce-scatter.2.cloned.1.call-update) | async-done | bytes 98320 | tf_op jit(solution)/shard_map/reduce_scatter | solution.py:101
  (50 shorter events, 7.7 us)
Async XLA Ops:
  7.2 5.2 %copy-start = (bf16[128,2048]{1,0:T(8,128)(2,1)S(1)}, bf16[128,2048]{1,0:T(8,128)(2,1)}, u32[]{:S(2)}) copy-start(bf16[128,2048]{1,0:T(8,128)(2,1)} %param.7) | copy-start | bytes 1572868
  7.2 101.4 %all-gather.7.cloned.1.call-start = ((), (), s32[]{:S(2)}) async-start(), calls=%async_computation.6 | async-start | bytes 3244032 | tf_op jit(solution)/shard_map/all_gather | solution.py:49
  7.9 174.6 %all-gather.9.cloned.1.call-start = ((), (), s32[]{:S(2)}) async-start(), calls=%async_computation.7 | async-start | bytes 3244032 | tf_op jit(solution)/shard_map/all_gather | solution.py:50
  8.7 258.8 %all-gather.11.cloned.1.call-start = ((), (), s32[]{:S(2)}) async-start(), calls=%async_computation.8 | async-start | bytes 3244032 | tf_op jit(solution)/shard_map/all_gather | solution.py:58
  14.2 12.0 %copy-start.5 = (f32[128,2]{0,1:T(2,128)S(1)}, f32[128,2]{0,1:T(2,128)}, u32[]{:S(2)}) copy-start(f32[128,2]{0,1:T(2,128)} %param.10) | copy-start | bytes 3076
  14.2 12.2 %copy-start.1 = (bf16[128,2048]{1,0:T(8,128)(2,1)S(1)}, bf16[128,2048]{1,0:T(8,128)(2,1)}, u32[]{:S(2)}) copy-start(bf16[128,2048]{1,0:T(8,128)(2,1)} %param.8) | copy-start | bytes 1572868
  14.2 50.6 %all-to-all-start = ((bf16[16,18,2048]{2,1,0:T(8,128)(2,1)}), bf16[16,18,2048]{2,1,0:T(8,128)(2,1)}, u32[]{:S(2)}, u32[]{:S(2)}) async-start(bf16[16,18,2048]{2,1,0:T(8,128)(2,1)} %reshape.96), calls=%async_computation | async-start | bytes 3145728 | tf_op jit(solution)/shard_map/all_to_all | solution.py:31
  64.7 42.7 %all-to-all-start.2 = ((bf16[16,18,2048]{2,1,0:T(8,128)(2,1)}), bf16[16,18,2048]{2,1,0:T(8,128)(2,1)S(1)}, u32[]{:S(2)}, u32[]{:S(2)}) async-start(bf16[16,18,2048]{2,1,0:T(8,128)(2,1)} %reshape.100), calls=%async_computation.2 | async-start | bytes 3145728 | tf_op jit(solution)/shard_map/all_to_all | solution.py:38
  68.9 426.5 %reduce-scatter.2.cloned.1.call-start = ((), (), s32[]{:S(2)}) async-start(), calls=%async_computation.5 | async-start | bytes 3244032 | tf_op jit(solution)/shard_map/reduce_scatter | solution.py:101
  108.6 73.9 %copy-start.3 = (bf16[288,2048]{1,0:T(8,128)(2,1)S(1)}, bf16[288,2048]{1,0:T(8,128)(2,1)}, u32[]{:S(2)}) copy-start(bf16[288,2048]{1,0:T(8,128)(2,1)} %reshape.97) | copy-start | bytes 3538948
  113.0 74.4 %copy-start.2 = (bf16[288,2048]{1,0:T(8,128)(2,1)S(1)}, bf16[288,2048]{1,0:T(8,128)(2,1)}, u32[]{:S(2)}) copy-start(bf16[288,2048]{1,0:T(8,128)(2,1)} %reshape.101) | copy-start | bytes 3538948
  186.6 0.8 copy-start.10
  191.0 76.5 %copy-start.11 = (bf16[288,768]{1,0:T(8,128)(2,1)S(1)}, bf16[288,768]{1,0:T(8,128)(2,1)}, u32[]{:S(2)}) copy-start(bf16[288,768]{1,0:T(8,128)(2,1)} %copy-done.10) | copy-start | bytes 1327108
  271.8 50.4 %all-to-all-start.1 = ((bf16[16,18,2048]{2,1,0:T(8,128)(2,1)}), bf16[16,18,2048]{2,1,0:T(8,128)(2,1)S(1)}, u32[]{:S(2)}, u32[]{:S(2)}) async-start(bf16[16,18,2048]{2,1,0:T(8,128)(2,1)} %reshape.98), calls=%async_computation.1 | async-start | bytes 3145728 | tf_op jit(solution)/shard_map/all_to_all | solution.py:72
  283.7 3.5 copy-start.7
  283.7 3.5 copy-start.8
  287.2 2.0 copy-start.6
  287.3 2.2 copy-start.9
  322.2 42.8 %all-to-all-start.3 = ((bf16[16,18,2048]{2,1,0:T(8,128)(2,1)}), bf16[16,18,2048]{2,1,0:T(8,128)(2,1)}, u32[]{:S(2)}, u32[]{:S(2)}) async-start(bf16[16,18,2048]{2,1,0:T(8,128)(2,1)} %reshape.102), calls=%async_computation.3 | async-start | bytes 3145728 | tf_op jit(solution)/shard_map/all_to_all | solution.py:79
  328.8 37.8 %copy-start.4 = (bf16[288,2048,1]{1,0,2:T(8,128)(2,1)S(1)}, bf16[288,2048,1]{1,0,2:T(8,128)(2,1)}, u32[]{:S(2)}) copy-start(bf16[288,2048,1]{1,0,2:T(8,128)(2,1)} %reshape.107) | copy-start | bytes 3538948
Sparse Core Ops, SparseCore 0:
  11.1 86.4 all-gather.6
  100.8 81.6 all-gather.8
  185.7 81.7 all-gather.10
  272.4 222.9 reduce-scatter.1
where the time goes:
time: 506 us; the launch traced here: 502 us
  waiting for transfers between devices  404 us (80%)
  starting transfers between devices  32.4 us (6%)
  matrix products  28.8 us (6%)
  local copies, waits for them, and re-layouts  19.9 us (4%)
  between operations  13.9 us (3%)
    reduce_scatter x1, waiting for transfers between devices, shards(): lax.psum_scatter(lax.dot_general(part_hidden, dy_rows, (((0,), (0,)), (()...  125 us
    all_gather x1, waiting for transfers between devices, shards(): weight_rows = lax.all_gather(down_weight[0], 'dp', axis=0, tiled=True)  76.5 us
    all_gather x1, waiting for transfers between devices, shards(): lax.all_gather(up_weight[0], 'dp', axis=0, tiled=True)  69.5 us
    all_to_all x1, waiting for transfers between devices, shards(): lax.all_to_all(grad_rows.reshape(groups, capacity, features), 'expert', s...  36.2 us
    all_to_all x1, waiting for transfers between devices, shards(): lax.all_to_all(send_grad.reshape(groups, capacity, features), 'expert', s...  36.1 us
    all_to_all x1, waiting for transfers between devices, shards(): lax.all_to_all(send_rows.reshape(groups, capacity, features), 'expert', s...  31.3 us
    all_to_all x1, waiting for transfers between devices, shards(): lax.all_to_all(output.reshape(groups, capacity, features), 'expert', spli...  28.2 us
    all_to_all x1, starting transfers between devices, shards(): lax.all_to_all(send_rows.reshape(groups, capacity, features), 'expert', s...  11.9 us
  transfers between devices with their start and end apart: 8, of which 7 were waited for; matrix products, arithmetic and copies ran while one was open for 10% of the time, Pallas kernels for 0%

commit v1 on v0

--- a/solution.py
+++ b/solution.py
@@ -27,35 +27,31 @@
     )
     send_rows = jnp.dot(placer_tok, tokens, preferred_element_type=jnp.float32).astype(jnp.bfloat16)
     send_grad = jnp.dot(placer, weighted, preferred_element_type=jnp.float32).astype(jnp.bfloat16)
-    recv_rows, recv_grad = (
-        lax.all_to_all(
-            send_rows.reshape(groups, capacity, features),
-            "expert",
-            split_axis=0,
-            concat_axis=0,
-            tiled=True,
-        ),
-        lax.all_to_all(
-            send_grad.reshape(groups, capacity, features),
-            "expert",
-            split_axis=0,
-            concat_axis=0,
-            tiled=True,
-        ),
+    recv_both = lax.all_to_all(
+        jnp.concatenate([send_rows, send_grad], axis=1).reshape(groups, capacity, 2 * features),
+        "expert",
+        split_axis=0,
+        concat_axis=0,
+        tiled=True,
+    ).reshape(slot_count, 2 * features)
+    x_rows = recv_both[:, :features]
+    dy_rows = recv_both[:, features:]
+    n_dp = lax.axis_size("dp")
+    hidden_units = gate_weight.shape[2]
+    rows_dp = down_weight.shape[1]
+    stacked = jnp.stack(
+        [gate_weight[0], up_weight[0], down_weight[0].reshape(gate_weight.shape[1], hidden_units)]
     )
-    x_rows = recv_rows.reshape(slot_count, features)
-    dy_rows = recv_grad.reshape(slot_count, features)
-    w_gate, w_up = (
-        lax.all_gather(gate_weight[0], "dp", axis=0, tiled=True),
-        lax.all_gather(up_weight[0], "dp", axis=0, tiled=True),
-    )
+    all_w = lax.all_gather(stacked[None], "dp", axis=0, tiled=True)
+    w_gate = all_w[:, 0].reshape(n_dp * gate_weight.shape[1], hidden_units)
+    w_up = all_w[:, 1].reshape(n_dp * gate_weight.shape[1], hidden_units)
+    weight_rows = all_w[:, 2].reshape(n_dp * rows_dp, features)
     gate_pre = jnp.dot(x_rows, w_gate, preferred_element_type=jnp.float32)
     up_pre = jnp.dot(x_rows, w_up, preferred_element_type=jnp.float32)
     sig_gate = jax.nn.sigmoid(gate_pre)
     active = gate_pre * sig_gate
     hidden = (active * up_pre).astype(jnp.bfloat16)
     contract = (((1,), (1,)), ((), ()))
-    weight_rows = lax.all_gather(down_weight[0], "dp", axis=0, tiled=True)
     part_hidden = hidden
     acc_part = jnp.dot(part_hidden, weight_rows, preferred_element_type=jnp.float32)
     back_part = lax.dot_general(dy_rows, weight_rows, contract, preferred_element_type=jnp.float32)
@@ -68,44 +64,41 @@
         lax.dot_general(grad_gate, w_gate, contract, preferred_element_type=jnp.float32)
         + lax.dot_general(grad_up, w_up, contract, preferred_element_type=jnp.float32)
     ).astype(jnp.bfloat16)
-    back_out, back_grad = (
-        lax.all_to_all(
-            output.reshape(groups, capacity, features),
-            "expert",
-            split_axis=0,
-            concat_axis=0,
-            tiled=True,
-        ),
-        lax.all_to_all(
-            grad_rows.reshape(groups, capacity, features),
-            "expert",
-            split_axis=0,
-            concat_axis=0,
-            tiled=True,
-        ),
-    )
+    back_both = lax.all_to_all(
+        jnp.concatenate([output, grad_rows], axis=1).reshape(groups, capacity, 2 * features),
+        "expert",
+        split_axis=0,
+        concat_axis=0,
+        tiled=True,
+    ).reshape(slot_count, 2 * features)
+    back_out = back_both[:, :features]
+    back_grad = back_both[:, features:]
     unplace = (((0,), (0,)), ((), ()))
     gathered = lax.dot_general(
-        placer, back_out.reshape(slot_count, features), unplace, preferred_element_type=jnp.float32
+        placer, back_out, unplace, preferred_element_type=jnp.float32
     )
     gathered = gathered.reshape(tok_count, choices_each, features)
     grad_tokens = lax.dot_general(
         placer_tok,
-        back_grad.reshape(slot_count, features),
+        back_grad,
         unplace,
         preferred_element_type=jnp.float32,
     ).astype(jnp.bfloat16)
     mixed_out = jnp.sum(router_probs[:, :, None] * gathered, axis=1).astype(jnp.bfloat16)
     grad_probs = jnp.sum(cotangent.astype(jnp.float32)[:, None, :] * gathered, axis=2)
     part_hidden = hidden
-    grad_down = lax.psum_scatter(
-        lax.dot_general(
-            part_hidden, dy_rows, (((0,), (0,)), ((), ())), preferred_element_type=jnp.float32
-        ).astype(jnp.bfloat16),
-        "dp",
-        scatter_dimension=0,
-        tiled=True,
-    )[None]
+    partial_value = lax.dot_general(
+        part_hidden, dy_rows, (((0,), (0,)), ((), ())), preferred_element_type=jnp.float32
+    ).astype(jnp.bfloat16)
+    grad_down = (
+        jnp.sum(
+            lax.all_to_all(
+                partial_value.reshape(n_dp, rows_dp, features), "dp", 0, 0, tiled=True
+            ).astype(jnp.float32),
+            axis=0,
+        )
+        .astype(jnp.bfloat16)[None]
+    )
     return (mixed_out, grad_tokens, grad_probs, grad_down)
 
 

time: 506 us -> 325 us (0.64)
  waiting for transfers between devices: 404 us -> 128 us
  blocking collectives: 0 us -> 85.3 us
  local copies, waits for them, and re-layouts: 19.9 us -> 46.4 us
  starting transfers between devices: 32.4 us -> 14.4 us
  other arithmetic: 2.54 us -> 14.4 us
  matrix products: 28.8 us -> 19.7 us
    all_gather x3 -> x1, waiting for transfers between devices: 146 us -> 9 us  [shards(): all_w = lax.all_gather(stacked[None], 'dp', axis=0, tiled=True)]
    reduce_scatter x1 -> x0, waiting for transfers between devices: 125 us -> none  [shards(): lax.psum_scatter(lax.dot_general(part_hidden, dy_rows, (((0,), (0,)), (()...]
    all_to_all x0 -> x1, blocking collectives: none -> 85.3 us  [shards(): lax.all_to_all(jnp.concatenate([send_rows, send_grad], axis=1).reshape(gr...]
    all_to_all x4 -> x2, starting transfers between devices: 32.3 us -> 14.4 us  [the longest x1 8.79 us: shards(): lax.all_to_all(jnp.concatenate([output, grad_rows], axis=1).reshape(group...]
    all_to_all x4 -> x2, waiting for transfers between devices: 132 us -> 119 us  [the longest x1 66.3 us: shards(): lax.all_to_all(jnp.concatenate([output, grad_rows], axis=1).reshape(group...]
    reduce_sum x0 -> x2, other arithmetic: none -> 8.72 us  [the longest x1 5.59 us: shards(): jnp.sum(router_probs[:, :, None] * gathered, axis=1).astype(jnp.bfloat16)]
    reshape x8 -> x5, local copies, waits for them, and re-layouts: 12.9 us -> 20.8 us  [the longest x1 4.35 us: shards(): jnp.concatenate([output, grad_rows], axis=1)]
    another operation x1 -> x3, local copies, waits for them, and re-layouts: 0.01 us -> 7.71 us  [the longest x1 6.62 us: shards(): weight_rows = all_w[:, 2].reshape(n_dp * rows_dp, features)]
  transfers between devices with their start and end apart: 8 -> 3, of which waited for: 7 -> 3; matrix products, arithmetic and copies ran while one was open for 10% -> 14% of each run, Pallas kernels for 0% -> 0%
where the time goes in v1:
time: 325 us; the launch traced here: 322 us
  waiting for transfers between devices  128 us (39%)
  blocking collectives  85.3 us (26%)
  local copies, waits for them, and re-layouts  46.4 us (14%)
  matrix products  19.7 us (6%)
  starting transfers between devices  14.4 us (4%)
  other arithmetic  14.4 us (4%)
  between operations  14.2 us (4%)
    all_to_all x1, blocking collectives, shards(): lax.all_to_all(jnp.concatenate([send_rows, send_grad], axis=1).reshape(gr...  85.3 us
    all_to_all x1, waiting for transfers between devices, shards(): lax.all_to_all(jnp.concatenate([output, grad_rows], axis=1).reshape(group...  66.3 us
    all_to_all x1, waiting for transfers between devices, shards(): lax.all_to_all(partial_value.reshape(n_dp, rows_dp, features), 'dp', 0, 0...  52.3 us
    all_gather x1, waiting for transfers between devices, shards(): all_w = lax.all_gather(stacked[None], 'dp', axis=0, tiled=True)  9 us
    all_to_all x1, starting transfers between devices, shards(): lax.all_to_all(jnp.concatenate([output, grad_rows], axis=1).reshape(group...  8.79 us
    slice x1, local copies, waits for them, and re-layouts, shards(): w_up = all_w[:, 1].reshape(n_dp * gate_weight.shape[1], hidden_units)  6.67 us
    another operation x1, local copies, waits for them, and re-layouts, shards(): weight_rows = all_w[:, 2].reshape(n_dp * rows_dp, features)  6.62 us
  transfers between devices with their start and end apart: 3, of which 3 were waited for; matrix products, arithmetic and copies ran while one was open for 14% of the time, Pallas kernels for 0%

profile of v1, /device:TPU:1, one launch (start us, length us, event | category | flops | bytes accessed | tf_op | source)
XLA Modules:
  0.0 322.1 jit_solution(15401786959059707836)
XLA Ops:
  7.2 1.1 stack_reshape_squeeze.3
  8.3 1.7 pad_maximum_fusion.2
  10.0 0.8 copy.39
  11.1 0.8 copy.38
  13.2 3.4 %mul.80 = f32[128,2,2048]{2,1,0:T(2,128)} broadcast(bf16[128,2048]{1,0:T(8,128)(2,1)} %param.8), dimensions={0,2} | broadcast | bytes 2621440 | tf_op jit(solution)/shard_map/mul | solution.py:24
  16.6 2.7 mul.81
  20.4 1.6 pad_maximum_fusion
  22.0 4.3 %reshape.73 = bf16[16,18,4096]{2,1,0:T(8,128)(2,1)} reshape(bf16[288,4096]{1,0:T(8,128)(2,1)} %pad_maximum_fusion) | data formatting | bytes 4718592 | tf_op jit(solution)/shard_map/reshape | solution.py:31
  26.3 85.3 %all_to_all.15 = bf16[16,18,4096]{2,1,0:T(8,128)(2,1)} all-to-all(bf16[16,18,4096]{2,1,0:T(8,128)(2,1)} %reshape.73), channel_id=1, replica_groups=mesh['dp'=32,'expert'=16] {'expert'}, dimensions={0} | all-to-all | bytes 4718592 | tf_op jit(solution)/shard_map/all_to_all | solution.py:30
  111.6 4.3 %reshape.74 = bf16[288,4096]{1,0:T(8,128)(2,1)} reshape(bf16[16,18,4096]{2,1,0:T(8,128)(2,1)} %all_to_all.15) | data formatting | bytes 4718592 | tf_op jit(solution)/shard_map/reshape | solution.py:36
  115.9 9.0 %all-gather.3.cloned.1.call-done = bf16[96,64,768]{2,1,0:T(8,128)(2,1)} async-done(((bf16[3,64,768]{2,1,0:T(8,128)(2,1)}), bf16[96,64,768]{2,1,0:T(8,128)(2,1)}) %all-gather.3.cloned.1.call-update) | async-done | bytes 9437200 | tf_op jit(solution)/shard_map/all_gather | solution.py:45
  124.9 6.7 %fusion.26 = (bf16[32,1,64,768]{3,2,1,0:T(8,128)(2,1)}, bf16[32,1,64,768]{3,2,1,0:T(8,128)(2,1)}, bf16[32,1,64,768]{3,2,1,0:T(8,128)(2,1)}) fusion(bf16[32,3,64,768]{3,2,1,0:T(8,128)(2,1)} %bitcast.37), kind=kLoop, calls=%fused_computation.50 | loop fusion | bytes 18874368 | tf_op jit(solution)/shard_map/slice | solution.py:47
  131.6 6.6 %reshape_squeeze.11 = bf16[768,2048]{1,0:T(8,128)(2,1)} reshape(bf16[32,1,64,768]{3,2,1,0:T(8,128)(2,1)} %get-tuple-element.21) | data formatting | bytes 6291456 | tf_op jit(solution)/shard_map/reshape;squeeze | solution.py:48
  138.2 3.5 %fusion.10 = f32[288,768]{1,0:T(8,128)S(1)} fusion(bf16[2048,768]{1,0:T(8,128)(2,1)} %bitcast.40, bf16[288,4096]{1,0:T(8,128)(2,1)} %reshape.74), kind=kOutput, calls=%fused_computation.21 | convolution fusion | flops 905969664 | bytes 5210112 | tf_op jit(solution)/shard_map/dot_general | solution.py:49
  142.1 1.1 fusion.6
  144.0 1.1 multiply_convert_fusion.4
  145.2 1.1 convolution_convert_fusion.2
  147.1 1.2 fusion.13
  148.3 1.1 fusion
  149.4 1.7 pad_maximum_fusion.1
  151.1 4.3 %reshape.75 = bf16[16,18,4096]{2,1,0:T(8,128)(2,1)} reshape(bf16[288,4096]{1,0:T(8,128)(2,1)} %pad_maximum_fusion.1) | data formatting | bytes 4718592 | tf_op jit(solution)/shard_map/reshape | solution.py:68
  155.4 8.8 %all-to-all-start.1 = ((bf16[16,18,4096]{2,1,0:T(8,128)(2,1)}), bf16[16,18,4096]{2,1,0:T(8,128)(2,1)}, u32[]{:S(2)}, u32[]{:S(2)}) async-start(bf16[16,18,4096]{2,1,0:T(8,128)(2,1)} %reshape.75), calls=%async_computation.1 | async-start | bytes 6291456 | tf_op jit(solution)/shard_map/all_to_all | solution.py:67
  164.2 4.8 %convolution_convert_fusion = bf16[768,2048]{1,0:T(8,128)(2,1)} fusion(bf16[288,768]{1,0:T(8,128)(2,1)S(1)} %get-tuple-element.23, bf16[288,4096]{1,0:T(8,128)(2,1)} %reshape.74), kind=kOutput, calls=%fused_computation | convolution fusion | flops 907542528 | bytes 4767744 | tf_op jit(solution)/shard_map/dot_general | solution.py:90
  169.0 66.3 %all-to-all-done.1 = bf16[16,18,4096]{2,1,0:T(8,128)(2,1)} async-done(((bf16[16,18,4096]{2,1,0:T(8,128)(2,1)}), bf16[16,18,4096]{2,1,0:T(8,128)(2,1)}, u32[]{:S(2)}, u32[]{:S(2)}) %all-to-all-start.1) | async-done | bytes 2359328 | tf_op jit(solution)/shard_map/all_to_all | solution.py:67
  235.3 5.6 %all-to-all-start.2 = ((bf16[32,24,2048]{2,1,0:T(8,128)(2,1)}), bf16[32,24,2048]{2,1,0:T(8,128)(2,1)}, u32[]{:S(2)}, u32[]{:S(2)}) async-start(bf16[32,24,2048]{2,1,0:T(8,128)(2,1)} %bitcast.42), calls=%async_computation.2 | async-start | bytes 6291456 | tf_op jit(solution)/shard_map/all_to_all | solution.py:95
  240.9 4.3 %reshape.76 = bf16[288,4096]{1,0:T(8,128)(2,1)} reshape(bf16[16,18,4096]{2,1,0:T(8,128)(2,1)} %all-to-all-done.1) | data formatting | bytes 4718592 | tf_op jit(solution)/shard_map/reshape | solution.py:73
  245.2 3.5 %multiply_reduce_fusion = (f32[256]{0:T(256)S(1)}, f32[256,2048]{1,0:T(8,128)}) fusion(f32[256,2048]{1,0:T(8,128)S(1)} %mul.81, bf16[288,4096]{1,0:T(8,128)(2,1)} %reshape.76, s32[256]{0:T(256)S(1)} %multiply_add_fusion.1), kind=kOutput, calls=%fused_computation.9 | convolution fusion | flops 303111936 | bytes 5376000 | tf_op jit(solution)/shard_map/dot_general | solution.py:77
  249.5 3.5 %reshape.77 = f32[128,2,2048]{2,1,0:T(2,128)} reshape(f32[256,2048]{1,0:T(8,128)} %get-tuple-element.26) | data formatting | bytes 4194304 | tf_op jit(solution)/shard_map/reshape | solution.py:80
  252.9 1.3 convolution_convert_fusion.4
  254.2 5.6 %multiply_reduce_fusion.1 = bf16[128,2048]{1,0:T(8,128)(2,1)} fusion(f32[128,2,2048]{2,1,0:T(2,128)} %reshape.77, f32[128,2]{1,0:T(8,128)S(1)} %copy.38), kind=kLoop, calls=%fused_computation.10 | loop fusion | flops 786432 | bytes 2622464 | tf_op jit(solution)/shard_map/reduce_sum | solution.py:87
  259.8 52.3 %all-to-all-done.2 = bf16[32,24,2048]{2,1,0:T(8,128)(2,1)} async-done(((bf16[32,24,2048]{2,1,0:T(8,128)(2,1)}), bf16[32,24,2048]{2,1,0:T(8,128)(2,1)}, u32[]{:S(2)}, u32[]{:S(2)}) %all-to-all-start.2) | async-done | bytes 3145760 | tf_op jit(solution)/shard_map/all_to_all | solution.py:95
  312.1 3.1 reduce_sum.61
  (36 shorter events, 5.4 us)
Async XLA Ops:
  7.2 12.2 %copy-start = (bf16[128,2048]{1,0:T(8,128)(2,1)S(1)}, bf16[128,2048]{1,0:T(8,128)(2,1)}, u32[]{:S(2)}) copy-start(bf16[128,2048]{1,0:T(8,128)(2,1)} %param.7) | copy-start | bytes 1572868
  7.2 117.7 %all-gather.3.cloned.1.call-start = ((), (), s32[]{:S(2)}) async-start(), calls=%async_computation.3 | async-start | bytes 9732096 | tf_op jit(solution)/shard_map/all_gather | solution.py:45
  16.6 2.7 copy-start.7
  138.2 3.5 %copy-start.5 = (bf16[768,2048]{1,0:T(8,128)(2,1)S(1)}, bf16[768,2048]{1,0:T(8,128)(2,1)}, u32[]{:S(2)}) copy-start(bf16[768,2048]{1,0:T(8,128)(2,1)} %reshape_squeeze.11) | copy-start | bytes 9437188
  138.2 3.9 %copy-start.6 = (bf16[288,4096]{1,0:T(8,128)(2,1)S(1)}, bf16[288,4096]{1,0:T(8,128)(2,1)}, u32[]{:S(2)}) copy-start(bf16[288,4096]{1,0:T(8,128)(2,1)} %reshape.74) | copy-start | bytes 7077892
  142.1 1.9 copy-start.3
  145.2 1.9 copy-start.4
  155.4 79.8 %all-to-all-start.1 = ((bf16[16,18,4096]{2,1,0:T(8,128)(2,1)}), bf16[16,18,4096]{2,1,0:T(8,128)(2,1)}, u32[]{:S(2)}, u32[]{:S(2)}) async-start(bf16[16,18,4096]{2,1,0:T(8,128)(2,1)} %reshape.75), calls=%async_computation.1 | async-start | bytes 6291456 | tf_op jit(solution)/shard_map/all_to_all | solution.py:67
  235.3 76.8 %all-to-all-start.2 = ((bf16[32,24,2048]{2,1,0:T(8,128)(2,1)}), bf16[32,24,2048]{2,1,0:T(8,128)(2,1)}, u32[]{:S(2)}, u32[]{:S(2)}) async-start(bf16[32,24,2048]{2,1,0:T(8,128)(2,1)} %bitcast.42), calls=%async_computation.2 | async-start | bytes 6291456 | tf_op jit(solution)/shard_map/all_to_all | solution.py:95
  248.7 4.2 %copy-start.2 = (bf16[288,4096]{1,0:T(8,128)(2,1)S(1)}, bf16[288,4096]{1,0:T(8,128)(2,1)}, u32[]{:S(2)}) copy-start(bf16[288,4096]{1,0:T(8,128)(2,1)} %reshape.76) | copy-start | bytes 7077892
  252.9 62.3 %copy-start.1 = (bf16[128,2048]{1,0:T(8,128)(2,1)S(1)}, bf16[128,2048]{1,0:T(8,128)(2,1)}, u32[]{:S(2)}) copy-start(bf16[128,2048]{1,0:T(8,128)(2,1)} %param.7) | copy-start | bytes 1572868
Sparse Core Ops, SparseCore 0:
  11.7 113.1 all-gather.2

commit v2 on v1

--- a/solution.py
+++ b/solution.py
@@ -1,7 +1,7 @@
 import jax
 import jax.numpy as jnp
 from jax import lax
-from jax.sharding import PartitionSpec as P
+from jax.sharding import Mesh, PartitionSpec as P
 
 
 def shards(tokens, cotangent, expert_ids, router_probs, gate_weight, up_weight, down_weight):
@@ -36,13 +36,13 @@
     ).reshape(slot_count, 2 * features)
     x_rows = recv_both[:, :features]
     dy_rows = recv_both[:, features:]
-    n_dp = lax.axis_size("dp")
+    n_dp = lax.axis_size(("dx", "dy"))
     hidden_units = gate_weight.shape[2]
     rows_dp = down_weight.shape[1]
     stacked = jnp.stack(
         [gate_weight[0], up_weight[0], down_weight[0].reshape(gate_weight.shape[1], hidden_units)]
     )
-    all_w = lax.all_gather(stacked[None], "dp", axis=0, tiled=True)
+    all_w = lax.all_gather(stacked[None], ("dx", "dy"), axis=0, tiled=True)
     w_gate = all_w[:, 0].reshape(n_dp * gate_weight.shape[1], hidden_units)
     w_up = all_w[:, 1].reshape(n_dp * gate_weight.shape[1], hidden_units)
     weight_rows = all_w[:, 2].reshape(n_dp * rows_dp, features)
@@ -53,6 +53,9 @@
     hidden = (active * up_pre).astype(jnp.bfloat16)
     contract = (((1,), (1,)), ((), ()))
     part_hidden = hidden
+    partial_value = lax.dot_general(
+        part_hidden, dy_rows, (((0,), (0,)), ((), ())), preferred_element_type=jnp.float32
+    ).astype(jnp.bfloat16)
     acc_part = jnp.dot(part_hidden, weight_rows, preferred_element_type=jnp.float32)
     back_part = lax.dot_general(dy_rows, weight_rows, contract, preferred_element_type=jnp.float32)
     output = acc_part.astype(jnp.bfloat16)
@@ -86,41 +89,28 @@
     ).astype(jnp.bfloat16)
     mixed_out = jnp.sum(router_probs[:, :, None] * gathered, axis=1).astype(jnp.bfloat16)
     grad_probs = jnp.sum(cotangent.astype(jnp.float32)[:, None, :] * gathered, axis=2)
-    part_hidden = hidden
-    partial_value = lax.dot_general(
-        part_hidden, dy_rows, (((0,), (0,)), ((), ())), preferred_element_type=jnp.float32
-    ).astype(jnp.bfloat16)
-    grad_down = (
-        jnp.sum(
-            lax.all_to_all(
-                partial_value.reshape(n_dp, rows_dp, features), "dp", 0, 0, tiled=True
-            ).astype(jnp.float32),
-            axis=0,
-        )
-        .astype(jnp.bfloat16)[None]
-    )
+    grad_down = lax.psum_scatter(
+        lax.psum_scatter(partial_value, "dx", scatter_dimension=0, tiled=True),
+        "dy",
+        scatter_dimension=0,
+        tiled=True,
+    )[None]
     return (mixed_out, grad_tokens, grad_probs, grad_down)
 
 
 def solution(mesh):
-    placed = (
-        P(("dp", "expert"), None),
-        P(("dp", "expert"), None),
-        P(("dp", "expert"), None),
-        P(("dp", "expert"), None),
-        P("expert", "dp", None),
-        P("expert", "dp", None),
-        P("expert", "dp", None),
+    n_x = 4
+    split = Mesh(
+        mesh.devices.reshape(n_x, mesh.shape["dp"] // n_x, mesh.shape["expert"]),
+        ("dx", "dy", "expert"),
     )
+    rows = P(("dx", "dy", "expert"), None)
+    experts = P("expert", ("dx", "dy"), None)
+    placed = (rows, rows, rows, rows, experts, experts, experts)
     return jax.shard_map(
         shards,
-        mesh=mesh,
+        mesh=split,
         in_specs=placed,
-        out_specs=(
-            P(("dp", "expert"), None),
-            P(("dp", "expert"), None),
-            P(("dp", "expert"), None),
-            P("expert", "dp", None),
-        ),
+        out_specs=(rows, rows, rows, experts),
         check_vma=False,
     )

time: 325 us -> 265 us (0.82)
  waiting for transfers between devices: 128 us -> 79.7 us
  starting transfers between devices: 14.4 us -> 9.51 us
  other arithmetic: 14.4 us -> 9.67 us
    all_to_all x1 -> x0, waiting for transfers between devices: 52.3 us -> none  [shards(): lax.all_to_all(partial_value.reshape(n_dp, rows_dp, features), 'dp', 0, 0...]
    reduce_scatter x0 -> x2, waiting for transfers between devices: none -> 10.6 us  [the longest x1 10.6 us: shards(): lax.psum_scatter(partial_value, 'dx', scatter_dimension=0, tiled=True)]
    all_to_all x1, waiting for transfers between devices: 66.3 us -> 60.1 us  [shards(): lax.all_to_all(jnp.concatenate([output, grad_rows], axis=1).reshape(group...]
    all_to_all x1 -> x0, starting transfers between devices: 5.59 us -> none  [shards(): lax.all_to_all(partial_value.reshape(n_dp, rows_dp, features), 'dp', 0, 0...]
  transfers between devices with their start and end apart: 3 -> 4, of which waited for: 3 -> 3; matrix products, arithmetic and copies ran while one was open for 14% -> 22% of each run, Pallas kernels for 0% -> 0%
where the time goes in v2:
time: 265 us; the launch traced here: 264 us
  blocking collectives  85.3 us (32%)
  waiting for transfers between devices  79.7 us (30%)
  local copies, waits for them, and re-layouts  45.6 us (17%)
  matrix products  20.1 us (8%)
  between operations  13.9 us (5%)
  other arithmetic  9.67 us (4%)
  starting transfers between devices  9.51 us (4%)
    all_to_all x1, blocking collectives, shards(): lax.all_to_all(jnp.concatenate([send_rows, send_grad], axis=1).reshape(gr...  85.3 us
    all_to_all x1, waiting for transfers between devices, shards(): lax.all_to_all(jnp.concatenate([output, grad_rows], axis=1).reshape(group...  60.1 us
    reduce_scatter x1, waiting for transfers between devices, shards(): lax.psum_scatter(partial_value, 'dx', scatter_dimension=0, tiled=True)  10.6 us
    all_to_all x1, starting transfers between devices, shards(): lax.all_to_all(jnp.concatenate([output, grad_rows], axis=1).reshape(group...  9.17 us
    all_gather x1, waiting for transfers between devices, shards(): all_w = lax.all_gather(stacked[None], ('dx', 'dy'), axis=0, tiled=True)  8.91 us
    another operation x1, local copies, waits for them, and re-layouts, shards(): weight_rows = all_w[:, 2].reshape(n_dp * rows_dp, features)  6.63 us
    mul x2, local copies, waits for them, and re-layouts, shards(): router_probs[:, :, None] * cotangent.astype(jnp.float32)[:, None, :]  6.15 us
    slice x1, local copies, waits for them, and re-layouts, shards(): w_up = all_w[:, 1].reshape(n_dp * gate_weight.shape[1], hidden_units)  5.45 us
  transfers between devices with their start and end apart: 4, of which 3 were waited for; matrix products, arithmetic and copies ran while one was open for 22% of the time, Pallas kernels for 0%

profile of v2, /device:TPU:1, one launch (start us, length us, event | category | flops | bytes accessed | tf_op | source)
XLA Modules:
  0.0 263.8 jit_solution(4616228854437065631)
XLA Ops:
  7.2 1.1 stack_reshape_squeeze.3
  8.3 1.7 pad_maximum_fusion.2
  10.1 0.8 copy.39
  11.1 0.8 copy.38
  13.2 3.4 %mul.80 = f32[128,2,2048]{2,1,0:T(2,128)} broadcast(bf16[128,2048]{1,0:T(8,128)(2,1)} %param.8), dimensions={0,2} | broadcast | bytes 2621440 | tf_op jit(solution)/shard_map/mul | solution.py:24
  16.7 2.7 %mul.81 = f32[256,2048]{1,0:T(8,128)S(1)} reshape(f32[128,2,2048]{2,1,0:T(2,128)} %mul.80) | data formatting | bytes 4194304 | tf_op jit(solution)/shard_map/mul | solution.py:24
  20.5 1.6 pad_maximum_fusion
  22.1 4.3 %reshape.70 = bf16[16,18,4096]{2,1,0:T(8,128)(2,1)} reshape(bf16[288,4096]{1,0:T(8,128)(2,1)} %pad_maximum_fusion) | data formatting | bytes 4718592 | tf_op jit(solution)/shard_map/reshape | solution.py:31
  26.4 85.3 %all_to_all.10 = bf16[16,18,4096]{2,1,0:T(8,128)(2,1)} all-to-all(bf16[16,18,4096]{2,1,0:T(8,128)(2,1)} %reshape.70), channel_id=1, replica_groups=mesh['dx'=4,'dy'=8,'expert'=16] {'expert'}, dimensions={0} | all-to-all | bytes 4718592 | tf_op jit(solution)/shard_map/all_to_all | solution.py:30
  111.7 4.3 %reshape.71 = bf16[288,4096]{1,0:T(8,128)(2,1)} reshape(bf16[16,18,4096]{2,1,0:T(8,128)(2,1)} %all_to_all.10) | data formatting | bytes 4718592 | tf_op jit(solution)/shard_map/reshape | solution.py:36
  116.0 8.9 %all-gather.3.cloned.1.call-done = bf16[96,64,768]{2,1,0:T(8,128)(2,1)} async-done(((bf16[3,64,768]{2,1,0:T(8,128)(2,1)}), bf16[96,64,768]{2,1,0:T(8,128)(2,1)}) %all-gather.3.cloned.1.call-update) | async-done | bytes 9437200 | tf_op jit(solution)/shard_map/all_gather | solution.py:45
  124.9 5.4 %fusion.26 = (bf16[32,1,64,768]{3,2,1,0:T(8,128)(2,1)S(1)}, bf16[32,1,64,768]{3,2,1,0:T(8,128)(2,1)}, bf16[32,1,64,768]{3,2,1,0:T(8,128)(2,1)S(1)}) fusion(bf16[32,3,64,768]{3,2,1,0:T(8,128)(2,1)} %bitcast.36), kind=kLoop, calls=%fused_computation.50 | loop fusion | bytes 18874368 | tf_op jit(solution)/shard_map/slice | solution.py:47
  130.4 1.1 fusion.10
  132.1 2.0 multiply_convert_fusion.4
  134.1 3.5 %convolution_convert_fusion = bf16[768,2048]{1,0:T(8,128)(2,1)} fusion(bf16[288,768]{1,0:T(8,128)(2,1)S(1)} %get-tuple-element.23, bf16[288,4096]{1,0:T(8,128)(2,1)S(1)} %copy-done.7), kind=kOutput, calls=%fused_computation | convolution fusion | flops 907542528 | bytes 4767744 | tf_op jit(solution)/shard_map/dot_general | solution.py:56
  137.7 6.6 %reshape_squeeze.11 = bf16[768,2048]{1,0:T(8,128)(2,1)} reshape(bf16[32,1,64,768]{3,2,1,0:T(8,128)(2,1)} %get-tuple-element.21) | data formatting | bytes 6291456 | tf_op jit(solution)/shard_map/reshape;squeeze | solution.py:48
  144.3 3.1 %convolution_convert_fusion.2 = bf16[288,2048]{1,0:T(8,128)(2,1)S(1)} fusion(bf16[288,768]{1,0:T(8,128)(2,1)S(1)} %get-tuple-element.23, bf16[768,2048]{1,0:T(8,128)(2,1)} %reshape_squeeze.11), kind=kOutput, calls=%fused_computation.4 | convolution fusion | flops 906559488 | bytes 4767744 | tf_op jit(solution)/shard_map/dot_general | solution.py:59
  147.9 1.1 fusion.6
  149.0 0.7 copy-done.5
  150.3 1.2 fusion.13
  151.5 0.9 copy-done.3
  152.3 1.1 fusion
  153.5 1.7 pad_maximum_fusion.1
  155.2 4.4 %reshape.72 = bf16[16,18,4096]{2,1,0:T(8,128)(2,1)} reshape(bf16[288,4096]{1,0:T(8,128)(2,1)} %pad_maximum_fusion.1) | data formatting | bytes 4718592 | tf_op jit(solution)/shard_map/reshape | solution.py:71
  159.6 9.2 %all-to-all-start.1 = ((bf16[16,18,4096]{2,1,0:T(8,128)(2,1)}), bf16[16,18,4096]{2,1,0:T(8,128)(2,1)}, u32[]{:S(2)}, u32[]{:S(2)}) async-start(bf16[16,18,4096]{2,1,0:T(8,128)(2,1)} %reshape.72), calls=%async_computation.1 | async-start | bytes 6291456 | tf_op jit(solution)/shard_map/all_to_all | solution.py:70
  169.0 10.6 %reduce-scatter.3.cloned.1.call-done = bf16[192,2048]{1,0:T(8,128)(2,1)} async-done(((bf16[768,2048]{1,0:T(8,128)(2,1)}), bf16[192,2048]{1,0:T(8,128)(2,1)}) %reduce-scatter.3.cloned.1.call-update) | async-done | bytes 786448 | tf_op jit(solution)/shard_map/reduce_scatter | solution.py:93
  179.7 60.1 %all-to-all-done.1 = bf16[16,18,4096]{2,1,0:T(8,128)(2,1)} async-done(((bf16[16,18,4096]{2,1,0:T(8,128)(2,1)}), bf16[16,18,4096]{2,1,0:T(8,128)(2,1)}, u32[]{:S(2)}, u32[]{:S(2)}) %all-to-all-start.1) | async-done | bytes 2359328 | tf_op jit(solution)/shard_map/all_to_all | solution.py:70
  239.8 4.4 %reshape.73 = bf16[288,4096]{1,0:T(8,128)(2,1)} reshape(bf16[16,18,4096]{2,1,0:T(8,128)(2,1)} %all-to-all-done.1) | data formatting | bytes 4718592 | tf_op jit(solution)/shard_map/reshape | solution.py:76
  244.1 3.4 %multiply_reduce_fusion = (f32[256]{0:T(256)S(1)}, f32[256,2048]{1,0:T(8,128)}) fusion(f32[256,2048]{1,0:T(8,128)S(1)} %mul.81, bf16[288,4096]{1,0:T(8,128)(2,1)} %reshape.73, s32[256]{0:T(256)S(1)} %multiply_add_fusion.1), kind=kOutput, calls=%fused_computation.9 | convolution fusion | flops 303111936 | bytes 5376000 | tf_op jit(solution)/shard_map/dot_general | solution.py:80
  248.3 2.5 reshape.74
  250.8 2.5 convolution_convert_fusion.4
  253.4 3.9 %multiply_reduce_fusion.1 = bf16[128,2048]{1,0:T(8,128)(2,1)} fusion(f32[128,2,2048]{2,1,0:T(2,128)S(1)} %reshape.74, f32[128,2]{1,0:T(8,128)S(1)} %copy.38), kind=kLoop, calls=%fused_computation.10 | loop fusion | flops 786432 | bytes 2622464 | tf_op jit(solution)/shard_map/reduce_sum | solution.py:90
  (49 shorter events, 5.3 us)
Async XLA Ops:
  7.2 12.3 %copy-start = (bf16[128,2048]{1,0:T(8,128)(2,1)S(1)}, bf16[128,2048]{1,0:T(8,128)(2,1)}, u32[]{:S(2)}) copy-start(bf16[128,2048]{1,0:T(8,128)(2,1)} %param.7) | copy-start | bytes 1572868
  7.2 117.8 %all-gather.3.cloned.1.call-start = ((), (), s32[]{:S(2)}) async-start(), calls=%async_computation.6 | async-start | bytes 9732096 | tf_op jit(solution)/shard_map/all_gather | solution.py:45
  10.0 169.6 %reduce-scatter.3.cloned.1.call-start = ((), (), s32[]{:S(2)}) async-start(), calls=%async_computation.4 | async-start | bytes 3932160 | tf_op jit(solution)/shard_map/reduce_scatter | solution.py:93
  16.7 2.7 %copy-start.9 = (s32[128,2]{0,1:T(2,128)S(1)}, s32[128,2]{0,1:T(2,128)}, u32[]{:S(2)}) copy-start(s32[128,2]{0,1:T(2,128)} %param.9) | copy-start | bytes 3076
  124.9 5.5 %copy-start.7 = (bf16[288,4096]{1,0:T(8,128)(2,1)S(1)}, bf16[288,4096]{1,0:T(8,128)(2,1)}, u32[]{:S(2)}) copy-start(bf16[288,4096]{1,0:T(8,128)(2,1)} %reshape.71) | copy-start | bytes 7077892
  130.4 1.7 copy-start.2
  130.4 3.7 %copy-start.4 = (bf16[32,1,64,768]{3,2,1,0:T(8,128)(2,1)}, bf16[32,1,64,768]{3,2,1,0:T(8,128)(2,1)S(1)}, u32[]{:S(2)}) copy-start(bf16[32,1,64,768]{3,2,1,0:T(8,128)(2,1)S(1)} %get-tuple-element.22) | copy-start | bytes 9437188
  131.5 2.6 copy-start.10
  144.3 3.1 %copy-start.6 = (bf16[768,2048]{1,0:T(8,128)(2,1)S(1)}, bf16[768,2048]{1,0:T(8,128)(2,1)}, u32[]{:S(2)}) copy-start(bf16[768,2048]{1,0:T(8,128)(2,1)} %reshape_squeeze.11) | copy-start | bytes 9437188
  144.3 3.6 %copy-start.8 = (bf16[288,4096]{1,0:T(8,128)(2,1)S(1)}, bf16[288,4096]{1,0:T(8,128)(2,1)}, u32[]{:S(2)}) copy-start(bf16[288,4096]{1,0:T(8,128)(2,1)} %reshape.71) | copy-start | bytes 7077892
  147.9 1.9 copy-start.5
  147.9 2.1 copy-start.11
  147.9 2.4 copy-start.12
  150.3 2.1 copy-start.3
  159.6 80.2 %all-to-all-start.1 = ((bf16[16,18,4096]{2,1,0:T(8,128)(2,1)}), bf16[16,18,4096]{2,1,0:T(8,128)(2,1)}, u32[]{:S(2)}, u32[]{:S(2)}) async-start(bf16[16,18,4096]{2,1,0:T(8,128)(2,1)} %reshape.72), calls=%async_computation.1 | async-start | bytes 6291456 | tf_op jit(solution)/shard_map/all_to_all | solution.py:70
  168.7 88.6 %reduce-scatter.5.cloned.1.call-start = ((), (), s32[]{:S(2)}) async-start(), calls=%async_computation.5 | async-start | bytes 884736 | tf_op jit(solution)/shard_map/reduce_scatter | solution.py:92
  248.3 9.0 %copy-start.1 = (bf16[128,2048]{1,0:T(8,128)(2,1)S(1)}, bf16[128,2048]{1,0:T(8,128)(2,1)}, u32[]{:S(2)}) copy-start(bf16[128,2048]{1,0:T(8,128)(2,1)} %param.7) | copy-start | bytes 1572868
Sparse Core Ops, SparseCore 0:
  11.7 113.1 all-gather.2
  137.8 41.7 reduce-scatter.2
  183.0 36.7 reduce-scatter.4

commit v3 on v2

v3 whole, which is shorter than its diff:
```python
import jax
import jax.numpy as jnp
from jax import lax
from jax.sharding import Mesh, PartitionSpec as P


def shards(tokens, cotangent, expert_ids, router_probs, gate_weight, up_weight, down_weight):
    tok_count = tokens.shape[0]
    features = tokens.shape[1]
    choices_each = expert_ids.shape[1]
    slot_total = tok_count * choices_each
    groups = lax.axis_size("expert")
    capacity = 9 * slot_total // (8 * groups)
    slot_count = groups * capacity
    n_dp = lax.axis_size(("dx", "dy"))
    rows_in = gate_weight.shape[1]
    hidden_units = gate_weight.shape[2]
    rows_dp = down_weight.shape[1]
    stacked = jnp.stack(
        [gate_weight[0], up_weight[0], down_weight[0].reshape(rows_in, hidden_units)]
    )
    all_w = lax.all_gather(stacked, ("dx", "dy"), axis=1, tiled=True)
    w_gate = all_w[0]
    w_up = all_w[1]
    weight_rows = all_w[2].reshape(n_dp * rows_dp, features)
    flat_ids = expert_ids.reshape(slot_total)
    member = (flat_ids[:, None] == jnp.arange(groups, dtype=jnp.int32)[None, :]).astype(jnp.int32)
    before = jnp.cumsum(member, axis=0) - member
    target = flat_ids * capacity + jnp.sum(before * member, axis=1)
    target_k = target.reshape(tok_count, choices_each)
    slot_ids = jnp.arange(slot_count, dtype=jnp.int32)[:, None]
    placers = [
        (target_k[None, :, k] == slot_ids).astype(jnp.bfloat16) for k in range(choices_each)
    ]
    placer_tok = sum(placers[1:], placers[0])
    cot32 = cotangent.astype(jnp.float32)
    send_rows = jnp.dot(placer_tok, tokens, preferred_element_type=jnp.float32)
    send_grad = sum(
        jnp.dot(
            placers[k],
            (router_probs[:, k, None] * cot32).astype(jnp.bfloat16),
            preferred_element_type=jnp.float32,
        )
        for k in range(choices_each)
    )
    recv_both = lax.all_to_all(
        jnp.concatenate([send_rows, send_grad], axis=1).astype(jnp.bfloat16),
        "expert",
        split_axis=0,
        concat_axis=0,
        tiled=True,
    )
    x_rows = recv_both[:, :features]
    dy_rows = recv_both[:, features:]
    gate_pre = jnp.dot(x_rows, w_gate, preferred_element_type=jnp.float32)
    up_pre = jnp.dot(x_rows, w_up, preferred_element_type=jnp.float32)
    sig_gate = jax.nn.sigmoid(gate_pre)
    active = gate_pre * sig_gate
    hidden = (active * up_pre).astype(jnp.bfloat16)
    contract = (((1,), (1,)), ((), ()))
    partial_value = lax.dot_general(
        hidden, dy_rows, (((0,), (0,)), ((), ())), preferred_element_type=jnp.float32
    ).astype(jnp.bfloat16)
    output = jnp.dot(hidden, weight_rows, preferred_element_type=jnp.float32).astype(jnp.bfloat16)
    back_out = lax.all_to_all(output, "expert", split_axis=0, concat_axis=0, tiled=True)
    back_part = lax.dot_general(dy_rows, weight_rows, contract, preferred_element_type=jnp.float32)
    grad_gate = (back_part * up_pre * sig_gate * (1.0 + gate_pre * (1.0 - sig_gate))).astype(
        jnp.bfloat16
    )
    grad_up = (back_part * active).astype(jnp.bfloat16)
    grad_rows = (
        lax.dot_general(grad_gate, w_gate, contract, preferred_element_type=jnp.float32)
        + lax.dot_general(grad_up, w_up, contract, preferred_element_type=jnp.float32)
    ).astype(jnp.bfloat16)
    back_grad = lax.all_to_all(grad_rows, "expert", split_axis=0, concat_axis=0, tiled=True)
    unplace = (((0,), (0,)), ((), ()))
    gathered = [
        lax.dot_general(placers[k], back_out, unplace, preferred_element_type=jnp.float32)
        for k in range(choices_each)
    ]
    mixed_out = sum(
        router_probs[:, k, None] * gathered[k] for k in range(choices_each)
    ).astype(jnp.bfloat16)
    grad_probs = jnp.stack(
        [jnp.sum(cot32 * gathered[k], axis=1) for k in range(choices_each)], axis=1
    )
    grad_tokens = lax.dot_general(
        placer_tok, back_grad, unplace, preferred_element_type=jnp.float32
    ).astype(jnp.bfloat16)
    grad_down = lax.psum_scatter(
        lax.psum_scatter(partial_value, "dx", scatter_dimension=0, tiled=True),
        "dy",
        scatter_dimension=0,
        tiled=True,
    )[None]
    return (mixed_out, grad_tokens, grad_probs, grad_down)


def solution(mesh):
    n_x = 4
    split = Mesh(
        mesh.devices.reshape(n_x, mesh.shape["dp"] // n_x, mesh.shape["expert"]),
        ("dx", "dy", "expert"),
    )
    rows = P(("dx", "dy", "expert"), None)
    experts = P("expert", ("dx", "dy"), None)
    placed = (rows, rows, rows, rows, experts, experts, experts)
    return jax.shard_map(
        shards,
        mesh=split,
        in_specs=placed,
        out_specs=(rows, rows, rows, experts),
        check_vma=False,
    )
```

time: 265 us -> 255 us (0.962)
  local copies, waits for them, and re-layouts: 45.6 us -> 24.8 us
  matrix products: 20.1 us -> 29.2 us
  other arithmetic: 9.67 us -> 5.44 us
  starting transfers between devices: 9.51 us -> 13.6 us
    reshape x6 -> x0, local copies, waits for them, and re-layouts: 20.1 us -> none  [the longest x1 4.38 us: shards(): jnp.concatenate([output, grad_rows], axis=1)]
    reduce_scatter x1, waiting for transfers between devices: 10.6 us -> 0.02 us  [shards(): lax.psum_scatter(partial_value, 'dx', scatter_dimension=0, tiled=True)]
    all_to_all x0 -> x5, local copies, waits for them, and re-layouts: none -> 8.47 us  [the longest x2 3.76 us: shards(): lax.all_to_all(grad_rows, 'expert', split_axis=0, concat_axis=0, tiled=True)]
    all_gather x1, waiting for transfers between devices: 8.91 us -> 16.9 us  [shards(): all_w = lax.all_gather(stacked, ('dx', 'dy'), axis=1, tiled=True)]
    mul x3 -> x1, local copies, waits for them, and re-layouts: 6.29 us -> 0.76 us  [shards(): router_probs[:, k, None] * cot32]
    all_to_all x1 -> x2, waiting for transfers between devices: 60.1 us -> 64.6 us  [the longest x1 37.3 us: shards(): lax.all_to_all(grad_rows, 'expert', split_axis=0, concat_axis=0, tiled=True)]
    all_to_all x1 -> x2, starting transfers between devices: 9.17 us -> 13.5 us  [the longest x1 9.19 us: shards(): lax.all_to_all(output, 'expert', split_axis=0, concat_axis=0, tiled=True)]
    reduce_sum x2 -> x0, other arithmetic: 3.96 us -> none  [the longest x1 3.93 us: shards(): jnp.sum(router_probs[:, :, None] * gathered, axis=1).astype(jnp.bfloat16)]
  transfers between devices with their start and end apart: 4 -> 5, of which waited for: 3 -> 3; matrix products, arithmetic and copies ran while one was open for 22% -> 14% of each run, Pallas kernels for 0% -> 0%
where the time goes in v3:
time: 255 us; the launch traced here: 254 us
  blocking collectives  85.1 us (33%)
  waiting for transfers between devices  82.3 us (32%)
  matrix products  29.2 us (11%)
  local copies, waits for them, and re-layouts  24.8 us (10%)
  between operations  14 us (5%)
  starting transfers between devices  13.6 us (5%)
  other arithmetic  5.44 us (2%)
    all_to_all x1, blocking collectives, shards(): lax.all_to_all(jnp.concatenate([send_rows, send_grad], axis=1).astype(jnp...  85.1 us
    all_to_all x1, waiting for transfers between devices, shards(): lax.all_to_all(grad_rows, 'expert', split_axis=0, concat_axis=0, tiled=True)  37.3 us
    all_to_all x1, waiting for transfers between devices, shards(): lax.all_to_all(output, 'expert', split_axis=0, concat_axis=0, tiled=True)  27.3 us
    all_gather x1, waiting for transfers between devices, shards(): all_w = lax.all_gather(stacked, ('dx', 'dy'), axis=1, tiled=True)  16.9 us
    all_to_all x1, starting transfers between devices, shards(): lax.all_to_all(output, 'expert', split_axis=0, concat_axis=0, tiled=True)  9.19 us
    another operation x1, local copies, waits for them, and re-layouts, shards(): weight_rows = all_w[2].reshape(n_dp * rows_dp, features)  6.68 us
  transfers between devices with their start and end apart: 5, of which 3 were waited for; matrix products, arithmetic and copies ran while one was open for 14% of the time, Pallas kernels for 0%

profile of v3, /device:TPU:1, one launch (start us, length us, event | category | flops | bytes accessed | tf_op | source)
XLA Modules:
  0.0 254.4 jit_solution(4812334428434100294)
XLA Ops:
  7.2 1.1 stack_reshape_squeeze.3
  8.4 1.7 pad_maximum_fusion.1
  10.1 0.8 copy.21
  11.2 0.6 reduce-window.6
  12.3 0.7 multiply_add_fusion
  13.0 0.8 slice_bitcast_fusion.8
  13.8 1.6 fusion.16
  16.8 1.4 concatenate.9
  18.2 1.7 pad_maximum_fusion
  20.0 85.1 %all_to_all.33 = bf16[16,18,4096]{2,1,0:T(8,128)(2,1)} all-to-all(bf16[16,18,4096]{2,1,0:T(8,128)(2,1)S(1)} %pad_maximum_fusion), channel_id=1, replica_groups=mesh['dx'=4,'dy'=8,'expert'=16] {'expert'}, dimensions={0} | all-to-all | bytes 4718592 | tf_op jit(solution)/shard_map/all_to_all | solution.py:46
  105.1 3.0 %all_to_all.23 = bf16[288,4096]{1,0:T(8,128)(2,1)S(1)} reshape(bf16[16,18,4096]{2,1,0:T(8,128)(2,1)} %all_to_all.33) | data formatting | bytes 4718592 | tf_op jit(solution)/shard_map/all_to_all | solution.py:46
  108.0 16.9 %all-gather.2.cloned.1.call-done = bf16[3,2048,768]{2,1,0:T(8,128)(2,1)} async-done(((bf16[3,64,768]{2,1,0:T(8,128)(2,1)}), bf16[3,2048,768]{2,1,0:T(8,128)(2,1)}) %all-gather.2.cloned.1.call-update) | async-done | bytes 9437200 | tf_op jit(solution)/shard_map/all_gather | solution.py:22
  125.0 3.0 %fusion.1 = f32[288,768]{1,0:T(8,128)S(1)} fusion(bf16[3,2048,768]{2,1,0:T(8,128)(2,1)} %all-gather.2.cloned.1.call-done, bf16[288,4096]{1,0:T(8,128)(2,1)S(1)} %all_to_all.23), kind=kOutput, calls=%fused_computation.7 | convolution fusion | flops 905969664 | bytes 5210112 | tf_op jit(solution)/shard_map/dot_general | solution.py:55
  127.9 4.2 %multiply_convert_fusion.2 = (bf16[288,768]{1,0:T(8,128)(2,1)S(1)}, f32[288,768]{1,0:T(8,128)}) fusion(f32[288,768]{1,0:T(8,128)S(1)} %fusion.1, bf16[3,2048,768]{2,1,0:T(8,128)(2,1)} %all-gather.2.cloned.1.call-done, bf16[288,4096]{1,0:T(8,128)(2,1)S(1)} %all_to_all.23), kind=kOutput, calls=%fused_computation.30 | convolution fusion | flops 907296768 | bytes 6537216 | tf_op jit(solution)/shard_map/dot_general | solution.py:56
  132.2 0.8 copy-done.7
  132.9 3.5 %convolution_convert_fusion = bf16[768,2048]{1,0:T(8,128)(2,1)} fusion(bf16[288,768]{1,0:T(8,128)(2,1)S(1)} %get-tuple-element.11, bf16[288,4096]{1,0:T(8,128)(2,1)S(1)} %all_to_all.23), kind=kOutput, calls=%fused_computation | convolution fusion | flops 907542528 | bytes 4767744 | tf_op jit(solution)/shard_map/dot_general | solution.py:61
  136.4 3.7 %slice.50 = bf16[1,2048,768]{2,1,0:T(8,128)(2,1)} slice(bf16[3,2048,768]{2,1,0:T(8,128)(2,1)} %all-gather.2.cloned.1.call-done), slice={[2:3], [0:2048], [0:768]} | slice | bytes 6291456 | tf_op jit(solution)/shard_map/slice | solution.py:25
  140.2 6.7 %reshape_squeeze.3 = bf16[768,2048]{1,0:T(8,128)(2,1)} reshape(bf16[1,2048,768]{2,1,0:T(8,128)(2,1)} %slice.50) | data formatting | bytes 6291456 | tf_op jit(solution)/shard_map/reshape;squeeze | solution.py:25
  146.9 3.0 %convolution_convert_fusion.2 = bf16[288,2048]{1,0:T(8,128)(2,1)S(1)} fusion(bf16[288,768]{1,0:T(8,128)(2,1)S(1)} %copy-done.8, bf16[768,2048]{1,0:T(8,128)(2,1)} %reshape_squeeze.3), kind=kOutput, calls=%fused_computation.12 | convolution fusion | flops 906559488 | bytes 4767744 | tf_op jit(solution)/shard_map/dot_general | solution.py:64
  149.8 1.3 all_to_all.24
  151.2 9.2 %all-to-all-start.1 = ((bf16[16,18,2048]{2,1,0:T(8,128)(2,1)}), bf16[16,18,2048]{2,1,0:T(8,128)(2,1)S(1)}, u32[]{:S(2)}, u32[]{:S(2)}) async-start(bf16[16,18,2048]{2,1,0:T(8,128)(2,1)} %all_to_all.24), calls=%async_computation.1 | async-start | bytes 3145728 | tf_op jit(solution)/shard_map/all_to_all | solution.py:65
  160.4 3.6 %fusion.10 = f32[288,768]{1,0:T(8,128)S(1)} fusion(bf16[768,2048]{1,0:T(8,128)(2,1)} %reshape_squeeze.3, bf16[288,4096]{1,0:T(8,128)(2,1)} %copy-done.4), kind=kOutput, calls=%fused_computation.24 | convolution fusion | flops 905969664 | bytes 5210112 | tf_op jit(solution)/shard_map/dot_general | solution.py:66
  164.0 3.1 %fusion = f32[288,2048]{1,0:T(8,128)S(1)} fusion(bf16[3,2048,768]{2,1,0:T(8,128)(2,1)} %all-gather.2.cloned.1.call-done, f32[288,768]{1,0:T(8,128)S(1)} %copy-done.6, f32[288,768]{1,0:T(8,128)S(1)} %fusion.10, f32[288,768]{1,0:T(8,128)S(1)} %copy-done.9), kind=kOutput, calls=%fused_computation.6 | convolution fusion | flops 908181504 | bytes 8159232 | tf_op jit(solution)/shard_map/dot_general | solution.py:72
  167.1 3.1 %fusion.4 = bf16[288,2048]{1,0:T(8,128)(2,1)S(1)} fusion(f32[288,2048]{1,0:T(8,128)S(1)} %fusion, bf16[3,2048,768]{2,1,0:T(8,128)(2,1)} %all-gather.2.cloned.1.call-done, f32[288,768]{1,0:T(8,128)S(1)} %fusion.10, f32[288,768]{1,0:T(8,128)S(1)} %copy-done.6), kind=kOutput, calls=%fused_computation.11 | convolution fusion | flops 908476416 | bytes 8454144 | tf_op jit(solution)/shard_map/dot_general | solution.py:73
  170.1 1.4 all_to_all.27
  171.5 27.3 %all-to-all-done.1 = bf16[16,18,2048]{2,1,0:T(8,128)(2,1)S(1)} async-done(((bf16[16,18,2048]{2,1,0:T(8,128)(2,1)}), bf16[16,18,2048]{2,1,0:T(8,128)(2,1)S(1)}, u32[]{:S(2)}, u32[]{:S(2)}) %all-to-all-start.1) | async-done | bytes 1179680 | tf_op jit(solution)/shard_map/all_to_all | solution.py:65
  198.9 4.3 %all-to-all-start.2 = ((bf16[16,18,2048]{2,1,0:T(8,128)(2,1)}), bf16[16,18,2048]{2,1,0:T(8,128)(2,1)}, u32[]{:S(2)}, u32[]{:S(2)}) async-start(bf16[16,18,2048]{2,1,0:T(8,128)(2,1)} %all_to_all.27), calls=%async_computation.2 | async-start | bytes 3145728 | tf_op jit(solution)/shard_map/all_to_all | solution.py:75
  203.3 0.7 reduce-scatter.5.cloned.1.call-update
  204.4 37.3 %all-to-all-done.2 = bf16[16,18,2048]{2,1,0:T(8,128)(2,1)} async-done(((bf16[16,18,2048]{2,1,0:T(8,128)(2,1)}), bf16[16,18,2048]{2,1,0:T(8,128)(2,1)}, u32[]{:S(2)}, u32[]{:S(2)}) %all-to-all-start.2) | async-done | bytes 1179680 | tf_op jit(solution)/shard_map/all_to_all | solution.py:75
  241.6 2.4 all_to_all.29
  244.5 1.5 fusion.7
  246.6 1.3 convolution_convert_fusion.3
  (42 shorter events, 3.9 us)
Async XLA Ops:
  7.2 9.2 %copy-start = (bf16[128,2048]{1,0:T(8,128)(2,1)S(1)}, bf16[128,2048]{1,0:T(8,128)(2,1)}, u32[]{:S(2)}) copy-start(bf16[128,2048]{1,0:T(8,128)(2,1)} %param.7) | copy-start | bytes 1572868
  7.2 8.2 %copy-start.1 = (bf16[128,2048]{1,0:T(8,128)(2,1)S(1)}, bf16[128,2048]{1,0:T(8,128)(2,1)}, u32[]{:S(2)}) copy-start(bf16[128,2048]{1,0:T(8,128)(2,1)} %param.8) | copy-start | bytes 1572868
  7.2 117.8 %all-gather.2.cloned.1.call-start = ((), (), s32[]{:S(2)}) async-start(), calls=%async_computation.5 | async-start | bytes 9732096 | tf_op jit(solution)/shard_map/all_gather | solution.py:22
  10.1 193.2 %reduce-scatter.3.cloned.1.call-start = ((), (), s32[]{:S(2)}) async-start(), calls=%async_computation.6 | async-start | bytes 3932160 | tf_op jit(solution)/shard_map/reduce_scatter | solution.py:91
  108.0 24.1 %copy-start.4 = (bf16[288,4096]{1,0:T(8,128)(2,1)}, bf16[288,4096]{1,0:T(8,128)(2,1)S(1)}, u32[]{:S(2)}) copy-start(bf16[288,4096]{1,0:T(8,128)(2,1)S(1)} %all_to_all.23) | copy-start | bytes 7077892
  127.9 4.2 %copy-start.5 = (f32[288,768]{1,0:T(8,128)}, f32[288,768]{1,0:T(8,128)S(1)}, u32[]{:S(2)}) copy-start(f32[288,768]{1,0:T(8,128)S(1)} %fusion.1) | copy-start | bytes 2654212
  132.2 0.8 copy-start.7
  140.2 6.7 %copy-start.8 = (bf16[288,768]{1,0:T(8,128)(2,1)S(1)}, bf16[288,768]{1,0:T(8,128)(2,1)}, u32[]{:S(2)}) copy-start(bf16[288,768]{1,0:T(8,128)(2,1)} %copy-done.7) | copy-start | bytes 1327108
  151.2 47.7 %all-to-all-start.1 = ((bf16[16,18,2048]{2,1,0:T(8,128)(2,1)}), bf16[16,18,2048]{2,1,0:T(8,128)(2,1)S(1)}, u32[]{:S(2)}, u32[]{:S(2)}) async-start(bf16[16,18,2048]{2,1,0:T(8,128)(2,1)} %all_to_all.24), calls=%async_computation.1 | async-start | bytes 3145728 | tf_op jit(solution)/shard_map/all_to_all | solution.py:65
  160.4 3.6 %copy-start.6 = (f32[288,768]{1,0:T(8,128)S(1)}, f32[288,768]{1,0:T(8,128)}, u32[]{:S(2)}) copy-start(f32[288,768]{1,0:T(8,128)} %copy-done.5) | copy-start | bytes 2654212
  160.4 3.6 %copy-start.9 = (f32[288,768]{1,0:T(8,128)S(1)}, f32[288,768]{1,0:T(8,128)}, u32[]{:S(2)}) copy-start(f32[288,768]{1,0:T(8,128)} %get-tuple-element.12) | copy-start | bytes 2654212
  198.9 42.8 %all-to-all-start.2 = ((bf16[16,18,2048]{2,1,0:T(8,128)(2,1)}), bf16[16,18,2048]{2,1,0:T(8,128)(2,1)}, u32[]{:S(2)}, u32[]{:S(2)}) async-start(bf16[16,18,2048]{2,1,0:T(8,128)(2,1)} %all_to_all.27), calls=%async_computation.2 | async-start | bytes 3145728 | tf_op jit(solution)/shard_map/all_to_all | solution.py:75
  203.2 44.7 %reduce-scatter.5.cloned.1.call-start = ((), (), s32[]{:S(2)}) async-start(), calls=%async_computation.7 | async-start | bytes 884736 | tf_op jit(solution)/shard_map/reduce_scatter | solution.py:90
  204.3 40.2 %copy-start.2 = (bf16[128,2048]{1,0:T(8,128)(2,1)S(1)}, bf16[128,2048]{1,0:T(8,128)(2,1)}, u32[]{:S(2)}) copy-start(bf16[128,2048]{1,0:T(8,128)(2,1)} %param.8) | copy-start | bytes 1572868
  244.0 2.6 %copy-start.3 = (bf16[288,2048]{1,0:T(8,128)(2,1)S(1)}, bf16[288,2048]{1,0:T(8,128)(2,1)}, u32[]{:S(2)}) copy-start(bf16[288,2048]{1,0:T(8,128)(2,1)} %all_to_all.29) | copy-start | bytes 3538948
Sparse Core Ops, SparseCore 0:
  11.7 113.1 all-gather.1
  136.6 41.7 reduce-scatter.2
  207.4 33.0 reduce-scatter.4

commit v4 on v3

--- a/solution.py
+++ b/solution.py
@@ -62,7 +62,9 @@
         hidden, dy_rows, (((0,), (0,)), ((), ())), preferred_element_type=jnp.float32
     ).astype(jnp.bfloat16)
     output = jnp.dot(hidden, weight_rows, preferred_element_type=jnp.float32).astype(jnp.bfloat16)
-    back_out = lax.all_to_all(output, "expert", split_axis=0, concat_axis=0, tiled=True)
+    back_out = lax.all_to_all(
+        output.reshape(groups, capacity, features), "expert", split_axis=0, concat_axis=0, tiled=True
+    )
     back_part = lax.dot_general(dy_rows, weight_rows, contract, preferred_element_type=jnp.float32)
     grad_gate = (back_part * up_pre * sig_gate * (1.0 + gate_pre * (1.0 - sig_gate))).astype(
         jnp.bfloat16
@@ -72,8 +74,12 @@
         lax.dot_general(grad_gate, w_gate, contract, preferred_element_type=jnp.float32)
         + lax.dot_general(grad_up, w_up, contract, preferred_element_type=jnp.float32)
     ).astype(jnp.bfloat16)
-    back_grad = lax.all_to_all(grad_rows, "expert", split_axis=0, concat_axis=0, tiled=True)
-    unplace = (((0,), (0,)), ((), ()))
+    back_grad = lax.all_to_all(
+        grad_rows.reshape(groups, capacity, features), "expert", split_axis=0, concat_axis=0, tiled=True
+    )
+    unplace = (((0, 1), (0, 1)), ((), ()))
+    placers = [p.reshape(groups, capacity, tok_count) for p in placers]
+    placer_tok = placer_tok.reshape(groups, capacity, tok_count)
     gathered = [
         lax.dot_general(placers[k], back_out, unplace, preferred_element_type=jnp.float32)
         for k in range(choices_each)

time: 255 us -> 252 us (0.988)
  waiting for transfers between devices: 82.3 us -> 72.5 us
  matrix products: 29.2 us -> 34.2 us
    all_to_all x4 -> x0, local copies, waits for them, and re-layouts: 5.5 us -> none  [the longest x2 3.76 us: shards(): lax.all_to_all(grad_rows, 'expert', split_axis=0, concat_axis=0, tiled=True)]
    all_gather x1, waiting for transfers between devices: 16.9 us -> 11.5 us  [shards(): all_w = lax.all_gather(stacked, ('dx', 'dy'), axis=1, tiled=True)]
    all_to_all x2, waiting for transfers between devices: 64.6 us -> 60.3 us  [the longest x1 35.1 us: shards(): lax.all_to_all(grad_rows.reshape(groups, capacity, features), 'expert', s...]
    reshape x0 -> x2, local copies, waits for them, and re-layouts: none -> 3.79 us  [the longest x1 2.45 us: shards(): grad_rows.reshape(groups, capacity, features)]
  transfers between devices with their start and end apart: 5 -> 5, of which waited for: 3 -> 3; matrix products, arithmetic and copies ran while one was open for 14% -> 19% of each run, Pallas kernels for 0% -> 0%
where the time goes in v4:
time: 252 us; the launch traced here: 251 us
  blocking collectives  85.1 us (34%)
  waiting for transfers between devices  72.5 us (29%)
  matrix products  34.2 us (14%)
  local copies, waits for them, and re-layouts  26.5 us (11%)
  between operations  13.9 us (6%)
  starting transfers between devices  13.7 us (5%)
  other arithmetic  5.45 us (2%)
    all_to_all x1, blocking collectives, shards(): lax.all_to_all(jnp.concatenate([send_rows, send_grad], axis=1).astype(jnp...  85.1 us
    all_to_all x1, waiting for transfers between devices, shards(): lax.all_to_all(grad_rows.reshape(groups, capacity, features), 'expert', s...  35.1 us
    all_to_all x1, waiting for transfers between devices, shards(): lax.all_to_all(output.reshape(groups, capacity, features), 'expert', spli...  25.3 us
    all_gather x1, waiting for transfers between devices, shards(): all_w = lax.all_gather(stacked, ('dx', 'dy'), axis=1, tiled=True)  11.5 us
    all_to_all x1, starting transfers between devices, shards(): lax.all_to_all(output.reshape(groups, capacity, features), 'expert', spli...  9.25 us
    another operation x1, local copies, waits for them, and re-layouts, shards(): weight_rows = all_w[2].reshape(n_dp * rows_dp, features)  6.61 us
  transfers between devices with their start and end apart: 5, of which 3 were waited for; matrix products, arithmetic and copies ran while one was open for 19% of the time, Pallas kernels for 0%

profile of v4, /device:TPU:1, one launch (start us, length us, event | category | flops | bytes accessed | tf_op | source)
XLA Modules:
  0.0 251.3 jit_solution(12789226397233801686)
XLA Ops:
  7.2 1.1 stack_reshape_squeeze.3
  8.4 1.7 pad_maximum_fusion.1
  10.1 0.8 copy.21
  12.3 0.7 multiply_add_fusion.1
  13.0 0.8 slice_bitcast_fusion.8
  13.8 1.6 fusion.17
  15.4 1.6 fusion.3
  17.0 1.4 concatenate.10
  18.4 1.5 convolution_convert_fusion.1
  19.9 2.4 concatenate.9
  22.3 1.7 pad_maximum_fusion
  24.0 85.1 %all_to_all.19 = bf16[16,18,4096]{2,1,0:T(8,128)(2,1)} all-to-all(bf16[16,18,4096]{2,1,0:T(8,128)(2,1)S(1)} %pad_maximum_fusion), channel_id=1, replica_groups=mesh['dx'=4,'dy'=8,'expert'=16] {'expert'}, dimensions={0} | all-to-all | bytes 4718592 | tf_op jit(solution)/shard_map/all_to_all | solution.py:46
  109.1 4.3 %all_to_all.13 = bf16[288,4096]{1,0:T(8,128)(2,1)} reshape(bf16[16,18,4096]{2,1,0:T(8,128)(2,1)} %all_to_all.19) | data formatting | bytes 4718592 | tf_op jit(solution)/shard_map/all_to_all | solution.py:46
  113.5 11.5 %all-gather.2.cloned.1.call-done = bf16[3,2048,768]{2,1,0:T(8,128)(2,1)} async-done(((bf16[3,64,768]{2,1,0:T(8,128)(2,1)}), bf16[3,2048,768]{2,1,0:T(8,128)(2,1)}) %all-gather.2.cloned.1.call-update) | async-done | bytes 9437200 | tf_op jit(solution)/shard_map/all_gather | solution.py:22
  125.0 3.5 %fusion.1 = f32[288,768]{1,0:T(8,128)S(1)} fusion(bf16[3,2048,768]{2,1,0:T(8,128)(2,1)} %all-gather.2.cloned.1.call-done, bf16[288,4096]{1,0:T(8,128)(2,1)} %all_to_all.13), kind=kOutput, calls=%fused_computation.7 | convolution fusion | flops 905969664 | bytes 5210112 | tf_op jit(solution)/shard_map/dot_general | solution.py:55
  128.5 3.9 %multiply_convert_fusion.2 = (bf16[288,768]{1,0:T(8,128)(2,1)S(1)}, f32[288,768]{1,0:T(8,128)}) fusion(f32[288,768]{1,0:T(8,128)S(1)} %fusion.1, bf16[3,2048,768]{2,1,0:T(8,128)(2,1)} %all-gather.2.cloned.1.call-done, bf16[288,4096]{1,0:T(8,128)(2,1)S(1)} %copy-done.2), kind=kOutput, calls=%fused_computation.33 | convolution fusion | flops 907296768 | bytes 6537216 | tf_op jit(solution)/shard_map/dot_general | solution.py:56
  132.4 0.8 copy-done.3
  133.2 3.5 %convolution_convert_fusion = bf16[768,2048]{1,0:T(8,128)(2,1)} fusion(bf16[288,768]{1,0:T(8,128)(2,1)S(1)} %get-tuple-element.11, bf16[288,4096]{1,0:T(8,128)(2,1)S(1)} %copy-done.2), kind=kOutput, calls=%fused_computation | convolution fusion | flops 907542528 | bytes 4767744 | tf_op jit(solution)/shard_map/dot_general | solution.py:61
  136.7 3.8 %slice.50 = bf16[1,2048,768]{2,1,0:T(8,128)(2,1)} slice(bf16[3,2048,768]{2,1,0:T(8,128)(2,1)} %all-gather.2.cloned.1.call-done), slice={[2:3], [0:2048], [0:768]} | slice | bytes 6291456 | tf_op jit(solution)/shard_map/slice | solution.py:25
  140.4 6.6 %reshape_squeeze.3 = bf16[768,2048]{1,0:T(8,128)(2,1)} reshape(bf16[1,2048,768]{2,1,0:T(8,128)(2,1)} %slice.50) | data formatting | bytes 6291456 | tf_op jit(solution)/shard_map/reshape;squeeze | solution.py:25
  147.0 3.1 %convolution_convert_fusion.2 = bf16[288,2048]{1,0:T(8,128)(2,1)S(1)} fusion(bf16[288,768]{1,0:T(8,128)(2,1)} %copy-done.3, bf16[768,2048]{1,0:T(8,128)(2,1)} %reshape_squeeze.3), kind=kOutput, calls=%fused_computation.12 | convolution fusion | flops 906559488 | bytes 4767744 | tf_op jit(solution)/shard_map/dot_general | solution.py:64
  150.1 1.3 reshape.84
  151.5 9.3 %all-to-all-start.1 = ((bf16[16,18,2048]{2,1,0:T(8,128)(2,1)}), bf16[16,18,2048]{2,1,0:T(8,128)(2,1)S(1)}, u32[]{:S(2)}, u32[]{:S(2)}) async-start(bf16[16,18,2048]{2,1,0:T(8,128)(2,1)} %reshape.84), calls=%async_computation.1 | async-start | bytes 3145728 | tf_op jit(solution)/shard_map/all_to_all | solution.py:65
  160.7 3.5 %fusion.11 = f32[288,768]{1,0:T(8,128)S(1)} fusion(bf16[768,2048]{1,0:T(8,128)(2,1)} %reshape_squeeze.3, bf16[288,4096]{1,0:T(8,128)(2,1)} %all_to_all.13), kind=kOutput, calls=%fused_computation.27 | convolution fusion | flops 905969664 | bytes 5210112 | tf_op jit(solution)/shard_map/dot_general | solution.py:68
  164.3 3.1 %fusion = f32[288,2048]{1,0:T(8,128)S(1)} fusion(bf16[3,2048,768]{2,1,0:T(8,128)(2,1)} %all-gather.2.cloned.1.call-done, f32[288,768]{1,0:T(8,128)S(1)} %fusion.1, f32[288,768]{1,0:T(8,128)S(1)} %fusion.11, f32[288,768]{1,0:T(8,128)S(1)} %copy-done.4), kind=kOutput, calls=%fused_computation.6 | convolution fusion | flops 908181504 | bytes 8159232 | tf_op jit(solution)/shard_map/dot_general | solution.py:74
  167.4 4.1 %fusion.4 = bf16[288,2048]{1,0:T(8,128)(2,1)} fusion(f32[288,2048]{1,0:T(8,128)S(1)} %fusion, bf16[3,2048,768]{2,1,0:T(8,128)(2,1)} %all-gather.2.cloned.1.call-done, f32[288,768]{1,0:T(8,128)S(1)} %fusion.11, f32[288,768]{1,0:T(8,128)S(1)} %fusion.1), kind=kOutput, calls=%fused_computation.11 | convolution fusion | flops 908476416 | bytes 8454144 | tf_op jit(solution)/shard_map/dot_general | solution.py:75
  171.6 2.5 reshape.85
  174.0 25.3 %all-to-all-done.1 = bf16[16,18,2048]{2,1,0:T(8,128)(2,1)S(1)} async-done(((bf16[16,18,2048]{2,1,0:T(8,128)(2,1)}), bf16[16,18,2048]{2,1,0:T(8,128)(2,1)S(1)}, u32[]{:S(2)}, u32[]{:S(2)}) %all-to-all-start.1) | async-done | bytes 1179680 | tf_op jit(solution)/shard_map/all_to_all | solution.py:65
  199.3 4.3 %all-to-all-start.2 = ((bf16[16,18,2048]{2,1,0:T(8,128)(2,1)}), bf16[16,18,2048]{2,1,0:T(8,128)(2,1)}, u32[]{:S(2)}, u32[]{:S(2)}) async-start(bf16[16,18,2048]{2,1,0:T(8,128)(2,1)} %reshape.85), calls=%async_computation.2 | async-start | bytes 3145728 | tf_op jit(solution)/shard_map/all_to_all | solution.py:77
  204.9 1.5 fusion.8
  207.0 35.1 %all-to-all-done.2 = bf16[16,18,2048]{2,1,0:T(8,128)(2,1)} async-done(((bf16[16,18,2048]{2,1,0:T(8,128)(2,1)}), bf16[16,18,2048]{2,1,0:T(8,128)(2,1)}, u32[]{:S(2)}, u32[]{:S(2)}) %all-to-all-start.2) | async-done | bytes 1179680 | tf_op jit(solution)/shard_map/all_to_all | solution.py:77
  242.0 2.8 %fusion.5 = bf16[128,2048]{1,0:T(8,128)(2,1)} fusion(bf16[16,18,2048]{2,1,0:T(8,128)(2,1)} %all-to-all-done.2, s32[128]{0:T(128)S(1)} %get-tuple-element.7, s32[16,18]{1,0:T(8,128)S(1)} %multiply_add_fusion, s32[128]{0:T(128)S(1)} %get-tuple-element.8), kind=kOutput, calls=%fused_computation.16 | convolution fusion | flops 151441408 | bytes 1706112 | tf_op jit(solution)/shard_map/dot_general | solution.py:93
  (31 shorter events, 3.4 us)
Async XLA Ops:
  7.2 11.2 %copy-start = (bf16[128,2048]{1,0:T(8,128)(2,1)S(1)}, bf16[128,2048]{1,0:T(8,128)(2,1)}, u32[]{:S(2)}) copy-start(bf16[128,2048]{1,0:T(8,128)(2,1)} %param.7) | copy-start | bytes 1572868
  7.2 8.2 %copy-start.1 = (bf16[128,2048]{1,0:T(8,128)(2,1)S(1)}, bf16[128,2048]{1,0:T(8,128)(2,1)}, u32[]{:S(2)}) copy-start(bf16[128,2048]{1,0:T(8,128)(2,1)} %param.8) | copy-start | bytes 1572868
  7.2 117.8 %all-gather.2.cloned.1.call-start = ((), (), s32[]{:S(2)}) async-start(), calls=%async_computation.5 | async-start | bytes 9732096 | tf_op jit(solution)/shard_map/all_gather | solution.py:22
  10.1 193.6 %reduce-scatter.3.cloned.1.call-start = ((), (), s32[]{:S(2)}) async-start(), calls=%async_computation.6 | async-start | bytes 3932160 | tf_op jit(solution)/shard_map/reduce_scatter | solution.py:97
  125.0 3.5 %copy-start.2 = (bf16[288,4096]{1,0:T(8,128)(2,1)S(1)}, bf16[288,4096]{1,0:T(8,128)(2,1)}, u32[]{:S(2)}) copy-start(bf16[288,4096]{1,0:T(8,128)(2,1)} %all_to_all.13) | copy-start | bytes 7077892
  132.4 0.8 copy-start.3
  151.5 47.8 %all-to-all-start.1 = ((bf16[16,18,2048]{2,1,0:T(8,128)(2,1)}), bf16[16,18,2048]{2,1,0:T(8,128)(2,1)S(1)}, u32[]{:S(2)}, u32[]{:S(2)}) async-start(bf16[16,18,2048]{2,1,0:T(8,128)(2,1)} %reshape.84), calls=%async_computation.1 | async-start | bytes 3145728 | tf_op jit(solution)/shard_map/all_to_all | solution.py:65
  160.7 3.5 %copy-start.4 = (f32[288,768]{1,0:T(8,128)S(1)}, f32[288,768]{1,0:T(8,128)}, u32[]{:S(2)}) copy-start(f32[288,768]{1,0:T(8,128)} %get-tuple-element.12) | copy-start | bytes 2654212
  199.3 42.8 %all-to-all-start.2 = ((bf16[16,18,2048]{2,1,0:T(8,128)(2,1)}), bf16[16,18,2048]{2,1,0:T(8,128)(2,1)}, u32[]{:S(2)}, u32[]{:S(2)}) async-start(bf16[16,18,2048]{2,1,0:T(8,128)(2,1)} %reshape.85), calls=%async_computation.2 | async-start | bytes 3145728 | tf_op jit(solution)/shard_map/all_to_all | solution.py:77
  203.6 41.2 %reduce-scatter.5.cloned.1.call-start = ((), (), s32[]{:S(2)}) async-start(), calls=%async_computation.7 | async-start | bytes 884736 | tf_op jit(solution)/shard_map/reduce_scatter | solution.py:96
Sparse Core Ops, SparseCore 0:
  11.7 113.1 all-gather.1
  136.8 41.7 reduce-scatter.2
  207.8 33.0 reduce-scatter.4

commit v5 on v4

--- a/solution.py
+++ b/solution.py
@@ -16,13 +16,12 @@
     rows_in = gate_weight.shape[1]
     hidden_units = gate_weight.shape[2]
     rows_dp = down_weight.shape[1]
-    stacked = jnp.stack(
-        [gate_weight[0], up_weight[0], down_weight[0].reshape(rows_in, hidden_units)]
+    stacked = jnp.concatenate(
+        [gate_weight[0], up_weight[0], down_weight[0].reshape(rows_in, hidden_units)], axis=1
     )
-    all_w = lax.all_gather(stacked, ("dx", "dy"), axis=1, tiled=True)
-    w_gate = all_w[0]
-    w_up = all_w[1]
-    weight_rows = all_w[2].reshape(n_dp * rows_dp, features)
+    all_w = lax.all_gather(stacked, ("dx", "dy"), axis=0, tiled=True)
+    w_both = all_w[:, : 2 * hidden_units]
+    weight_rows = all_w[:, 2 * hidden_units :].reshape(n_dp * rows_dp, features)
     flat_ids = expert_ids.reshape(slot_total)
     member = (flat_ids[:, None] == jnp.arange(groups, dtype=jnp.int32)[None, :]).astype(jnp.int32)
     before = jnp.cumsum(member, axis=0) - member
@@ -52,8 +51,9 @@
     )
     x_rows = recv_both[:, :features]
     dy_rows = recv_both[:, features:]
-    gate_pre = jnp.dot(x_rows, w_gate, preferred_element_type=jnp.float32)
-    up_pre = jnp.dot(x_rows, w_up, preferred_element_type=jnp.float32)
+    both_pre = jnp.dot(x_rows, w_both, preferred_element_type=jnp.float32)
+    gate_pre = both_pre[:, :hidden_units]
+    up_pre = both_pre[:, hidden_units:]
     sig_gate = jax.nn.sigmoid(gate_pre)
     active = gate_pre * sig_gate
     hidden = (active * up_pre).astype(jnp.bfloat16)
@@ -70,9 +70,11 @@
         jnp.bfloat16
     )
     grad_up = (back_part * active).astype(jnp.bfloat16)
-    grad_rows = (
-        lax.dot_general(grad_gate, w_gate, contract, preferred_element_type=jnp.float32)
-        + lax.dot_general(grad_up, w_up, contract, preferred_element_type=jnp.float32)
+    grad_rows = lax.dot_general(
+        jnp.concatenate([grad_gate, grad_up], axis=1),
+        w_both,
+        contract,
+        preferred_element_type=jnp.float32,
     ).astype(jnp.bfloat16)
     back_grad = lax.all_to_all(
         grad_rows.reshape(groups, capacity, features), "expert", split_axis=0, concat_axis=0, tiled=True

time: 252 us -> 251 us (level)
  matrix products: 34.2 us -> 29.2 us
  waiting for transfers between devices: 72.5 us -> 77.5 us
    another operation x3 -> x2, local copies, waits for them, and re-layouts: 7.74 us -> 1.13 us  [the longest x1 1.12 us: shards(): down_weight[0].reshape(rows_in, hidden_units)]
    reshape x0 -> x1, local copies, waits for them, and re-layouts: none -> 6.61 us  [shards(): weight_rows = all_w[:, 2 * hidden_units:].reshape(n_dp * rows_dp, features)]
    all_to_all x1, waiting for transfers between devices: 25.3 us -> 30.3 us  [shards(): lax.all_to_all(output.reshape(groups, capacity, features), 'expert', spli...]
    dot_general x4 -> x2, matrix products: 14.7 us -> 11.1 us  [the longest x1 5.85 us: shards(): lax.dot_general(jnp.concatenate([grad_gate, grad_up], axis=1), w_both, co...]
  transfers between devices with their start and end apart: 5 -> 5, of which waited for: 3 -> 3; matrix products, arithmetic and copies ran while one was open for 19% -> 13% of each run, Pallas kernels for 0% -> 0%
where the time goes in v5:
time: 251 us; the launch traced here: 250 us
  blocking collectives  85.1 us (34%)
  waiting for transfers between devices  77.5 us (31%)
  matrix products  29.2 us (12%)
  local copies, waits for them, and re-layouts  25.7 us (10%)
  between operations  13.9 us (6%)
  starting transfers between devices  13.2 us (5%)
  other arithmetic  5.43 us (2%)
    all_to_all x1, blocking collectives, shards(): lax.all_to_all(jnp.concatenate([send_rows, send_grad], axis=1).astype(jnp...  85.1 us
    all_to_all x1, waiting for transfers between devices, shards(): lax.all_to_all(grad_rows.reshape(groups, capacity, features), 'expert', s...  35.1 us
    all_to_all x1, waiting for transfers between devices, shards(): lax.all_to_all(output.reshape(groups, capacity, features), 'expert', spli...  30.3 us
    all_gather x1, waiting for transfers between devices, shards(): all_w = lax.all_gather(stacked, ('dx', 'dy'), axis=0, tiled=True)  11.5 us
    all_to_all x1, starting transfers between devices, shards(): lax.all_to_all(output.reshape(groups, capacity, features), 'expert', spli...  8.77 us
    reshape x1, local copies, waits for them, and re-layouts, shards(): weight_rows = all_w[:, 2 * hidden_units:].reshape(n_dp * rows_dp, features)  6.61 us
    dot_general x1, matrix products, shards(): lax.dot_general(jnp.concatenate([grad_gate, grad_up], axis=1), w_both, co...  5.85 us
    dot_general x1, matrix products, shards(): both_pre = jnp.dot(x_rows, w_both, preferred_element_type=jnp.float32)  5.27 us
  transfers between devices with their start and end apart: 5, of which 3 were waited for; matrix products, arithmetic and copies ran while one was open for 13% of the time, Pallas kernels for 0%

profile of v5, /device:TPU:1, one launch (start us, length us, event | category | flops | bytes accessed | tf_op | source)
XLA Modules:
  0.0 250.0 jit_solution(10408505769768328696)
XLA Ops:
  7.2 1.1 reshape_squeeze.3
  8.4 1.7 pad_maximum_fusion.1
  10.1 0.8 copy.21
  11.2 0.6 reduce-window.6
  12.3 0.7 multiply_add_fusion.1
  13.0 0.8 slice_bitcast_fusion
  13.8 1.6 fusion.22
  15.4 1.6 fusion.7
  16.9 1.4 concatenate.16
  18.4 1.5 convolution_convert_fusion.1
  19.9 2.4 concatenate.15
  22.3 1.7 pad_maximum_fusion
  24.0 85.1 %all_to_all.19 = bf16[16,18,4096]{2,1,0:T(8,128)(2,1)} all-to-all(bf16[16,18,4096]{2,1,0:T(8,128)(2,1)S(1)} %pad_maximum_fusion), channel_id=1, replica_groups=mesh['dx'=4,'dy'=8,'expert'=16] {'expert'}, dimensions={0} | all-to-all | bytes 4718592 | tf_op jit(solution)/shard_map/all_to_all | solution.py:45
  109.1 4.3 %all_to_all.13 = bf16[288,4096]{1,0:T(8,128)(2,1)} reshape(bf16[16,18,4096]{2,1,0:T(8,128)(2,1)} %all_to_all.19) | data formatting | bytes 4718592 | tf_op jit(solution)/shard_map/all_to_all | solution.py:45
  113.5 11.5 %all-gather.2.cloned.1.call-done = bf16[2048,2304]{1,0:T(8,128)(2,1)} async-done(((bf16[64,2304]{1,0:T(8,128)(2,1)}), bf16[2048,2304]{1,0:T(8,128)(2,1)}) %all-gather.2.cloned.1.call-update) | async-done | bytes 9437200 | tf_op jit(solution)/shard_map/all_gather | solution.py:22
  124.9 3.7 %slice.55 = bf16[2048,768]{1,0:T(8,128)(2,1)} slice(bf16[2048,2304]{1,0:T(8,128)(2,1)} %all-gather.2.cloned.1.call-done), slice={[0:2048], [1536:2304]} | slice | bytes 6291456 | tf_op jit(solution)/shard_map/slice | solution.py:24
  128.7 6.6 %reshape.87 = bf16[768,2048]{1,0:T(8,128)(2,1)} reshape(bf16[2048,768]{1,0:T(8,128)(2,1)} %slice.55) | data formatting | bytes 6291456 | tf_op jit(solution)/shard_map/reshape | solution.py:24
  135.3 5.3 %fusion.2 = f32[288,1536]{1,0:T(8,128)S(1)} fusion(bf16[2048,2304]{1,0:T(8,128)(2,1)} %all-gather.2.cloned.1.call-done, bf16[288,4096]{1,0:T(8,128)(2,1)} %all_to_all.13), kind=kOutput, calls=%fused_computation.2 | convolution fusion | flops 1811939328 | bytes 9240576 | tf_op jit(solution)/shard_map/dot_general | solution.py:54
  140.6 2.2 multiply_convert_fusion.1
  142.7 3.5 %convolution_convert_fusion = bf16[768,2048]{1,0:T(8,128)(2,1)} fusion(bf16[288,768]{1,0:T(8,128)(2,1)S(1)} %get-tuple-element.9, bf16[288,4096]{1,0:T(8,128)(2,1)S(1)} %copy-done.3), kind=kOutput, calls=%fused_computation.4 | convolution fusion | flops 907542528 | bytes 4767744 | tf_op jit(solution)/shard_map/dot_general | solution.py:61
  146.2 3.0 %convolution_convert_fusion.2 = bf16[288,2048]{1,0:T(8,128)(2,1)S(1)} fusion(bf16[288,768]{1,0:T(8,128)(2,1)S(1)} %get-tuple-element.9, bf16[768,2048]{1,0:T(8,128)(2,1)} %reshape.87), kind=kOutput, calls=%fused_computation.10 | convolution fusion | flops 906559488 | bytes 4767744 | tf_op jit(solution)/shard_map/dot_general | solution.py:64
  149.3 1.4 reshape.88
  150.7 8.8 %all-to-all-start.1 = ((bf16[16,18,2048]{2,1,0:T(8,128)(2,1)}), bf16[16,18,2048]{2,1,0:T(8,128)(2,1)S(1)}, u32[]{:S(2)}, u32[]{:S(2)}) async-start(bf16[16,18,2048]{2,1,0:T(8,128)(2,1)} %reshape.88), calls=%async_computation.1 | async-start | bytes 3145728 | tf_op jit(solution)/shard_map/all_to_all | solution.py:65
  159.4 5.9 %fusion.4 = bf16[288,2048]{1,0:T(8,128)(2,1)} fusion(bf16[2048,2304]{1,0:T(8,128)(2,1)} %all-gather.2.cloned.1.call-done, bf16[288,768]{1,0:T(8,128)(2,1)S(1)} %copy-done.4, bf16[288,768]{1,0:T(8,128)(2,1)S(1)} %get-tuple-element.6), kind=kOutput, calls=%fused_computation.7 | convolution fusion | flops 1814298624 | bytes 8355840 | tf_op jit(solution)/shard_map/dot_general | solution.py:73
  165.3 2.4 reshape.89
  167.7 30.3 %all-to-all-done.1 = bf16[16,18,2048]{2,1,0:T(8,128)(2,1)S(1)} async-done(((bf16[16,18,2048]{2,1,0:T(8,128)(2,1)}), bf16[16,18,2048]{2,1,0:T(8,128)(2,1)S(1)}, u32[]{:S(2)}, u32[]{:S(2)}) %all-to-all-start.1) | async-done | bytes 1179680 | tf_op jit(solution)/shard_map/all_to_all | solution.py:65
  198.0 4.3 %all-to-all-start.2 = ((bf16[16,18,2048]{2,1,0:T(8,128)(2,1)}), bf16[16,18,2048]{2,1,0:T(8,128)(2,1)}, u32[]{:S(2)}, u32[]{:S(2)}) async-start(bf16[16,18,2048]{2,1,0:T(8,128)(2,1)} %reshape.89), calls=%async_computation.2 | async-start | bytes 3145728 | tf_op jit(solution)/shard_map/all_to_all | solution.py:79
  202.3 0.7 reduce-scatter.5.cloned.1.call-update
  203.6 1.5 fusion.12
  205.1 0.6 pad_maximum_fusion.2
  205.7 35.1 %all-to-all-done.2 = bf16[16,18,2048]{2,1,0:T(8,128)(2,1)} async-done(((bf16[16,18,2048]{2,1,0:T(8,128)(2,1)}), bf16[16,18,2048]{2,1,0:T(8,128)(2,1)}, u32[]{:S(2)}, u32[]{:S(2)}) %all-to-all-start.2) | async-done | bytes 1179680 | tf_op jit(solution)/shard_map/all_to_all | solution.py:79
  240.7 2.8 %fusion.8 = bf16[128,2048]{1,0:T(8,128)(2,1)} fusion(bf16[16,18,2048]{2,1,0:T(8,128)(2,1)} %all-to-all-done.2, s32[128]{0:T(128)S(1)} %get-tuple-element.10, s32[16,18]{1,0:T(8,128)S(1)} %multiply_add_fusion, s32[128]{0:T(128)S(1)} %get-tuple-element.11), kind=kOutput, calls=%fused_computation.14 | convolution fusion | flops 151441408 | bytes 1706112 | tf_op jit(solution)/shard_map/dot_general | solution.py:95
  (29 shorter events, 1.6 us)
Async XLA Ops:
  7.2 11.2 %copy-start = (bf16[128,2048]{1,0:T(8,128)(2,1)S(1)}, bf16[128,2048]{1,0:T(8,128)(2,1)}, u32[]{:S(2)}) copy-start(bf16[128,2048]{1,0:T(8,128)(2,1)} %param.7) | copy-start | bytes 1572868
  7.2 8.2 %copy-start.1 = (bf16[128,2048]{1,0:T(8,128)(2,1)S(1)}, bf16[128,2048]{1,0:T(8,128)(2,1)}, u32[]{:S(2)}) copy-start(bf16[128,2048]{1,0:T(8,128)(2,1)} %param.8) | copy-start | bytes 1572868
  7.2 117.8 %all-gather.2.cloned.1.call-start = ((), (), s32[]{:S(2)}) async-start(), calls=%async_computation.5 | async-start | bytes 9732096 | tf_op jit(solution)/shard_map/all_gather | solution.py:22
  10.1 192.3 %reduce-scatter.3.cloned.1.call-start = ((), (), s32[]{:S(2)}) async-start(), calls=%async_computation.6 | async-start | bytes 3932160 | tf_op jit(solution)/shard_map/reduce_scatter | solution.py:99
  135.3 5.3 %copy-start.2 = (bf16[768,2048]{1,0:T(8,128)(2,1)S(1)}, bf16[768,2048]{1,0:T(8,128)(2,1)}, u32[]{:S(2)}) copy-start(bf16[768,2048]{1,0:T(8,128)(2,1)} %reshape.87) | copy-start | bytes 9437188
  135.3 5.3 %copy-start.3 = (bf16[288,4096]{1,0:T(8,128)(2,1)S(1)}, bf16[288,4096]{1,0:T(8,128)(2,1)}, u32[]{:S(2)}) copy-start(bf16[288,4096]{1,0:T(8,128)(2,1)} %all_to_all.13) | copy-start | bytes 7077892
  149.3 10.2 %copy-start.4 = (bf16[288,768]{1,0:T(8,128)(2,1)S(1)}, bf16[288,768]{1,0:T(8,128)(2,1)}, u32[]{:S(2)}) copy-start(bf16[288,768]{1,0:T(8,128)(2,1)} %get-tuple-element.7) | copy-start | bytes 1327108
  150.7 47.3 %all-to-all-start.1 = ((bf16[16,18,2048]{2,1,0:T(8,128)(2,1)}), bf16[16,18,2048]{2,1,0:T(8,128)(2,1)S(1)}, u32[]{:S(2)}, u32[]{:S(2)}) async-start(bf16[16,18,2048]{2,1,0:T(8,128)(2,1)} %reshape.88), calls=%async_computation.1 | async-start | bytes 3145728 | tf_op jit(solution)/shard_map/all_to_all | solution.py:65
  198.0 42.8 %all-to-all-start.2 = ((bf16[16,18,2048]{2,1,0:T(8,128)(2,1)}), bf16[16,18,2048]{2,1,0:T(8,128)(2,1)}, u32[]{:S(2)}, u32[]{:S(2)}) async-start(bf16[16,18,2048]{2,1,0:T(8,128)(2,1)} %reshape.89), calls=%async_computation.2 | async-start | bytes 3145728 | tf_op jit(solution)/shard_map/all_to_all | solution.py:79
  202.3 41.2 %reduce-scatter.5.cloned.1.call-start = ((), (), s32[]{:S(2)}) async-start(), calls=%async_computation.7 | async-start | bytes 884736 | tf_op jit(solution)/shard_map/reduce_scatter | solution.py:98
Sparse Core Ops, SparseCore 0:
  11.7 113.1 all-gather.1
  146.3 41.7 reduce-scatter.2
  206.5 33.4 reduce-scatter.4

commit v6 on v5

--- a/solution.py
+++ b/solution.py
@@ -58,8 +58,15 @@
     active = gate_pre * sig_gate
     hidden = (active * up_pre).astype(jnp.bfloat16)
     contract = (((1,), (1,)), ((), ()))
+    n_x = lax.axis_size("dx")
+    n_y = lax.axis_size("dy")
+    hidden_yx = (
+        hidden.reshape(slot_count, n_x, n_y, rows_dp)
+        .transpose(0, 2, 1, 3)
+        .reshape(slot_count, n_dp * rows_dp)
+    )
     partial_value = lax.dot_general(
-        hidden, dy_rows, (((0,), (0,)), ((), ())), preferred_element_type=jnp.float32
+        hidden_yx, dy_rows, (((0,), (0,)), ((), ())), preferred_element_type=jnp.float32
     ).astype(jnp.bfloat16)
     output = jnp.dot(hidden, weight_rows, preferred_element_type=jnp.float32).astype(jnp.bfloat16)
     back_out = lax.all_to_all(
@@ -96,8 +103,8 @@
         placer_tok, back_grad, unplace, preferred_element_type=jnp.float32
     ).astype(jnp.bfloat16)
     grad_down = lax.psum_scatter(
-        lax.psum_scatter(partial_value, "dx", scatter_dimension=0, tiled=True),
-        "dy",
+        lax.psum_scatter(partial_value, "dy", scatter_dimension=0, tiled=True),
+        "dx",
         scatter_dimension=0,
         tiled=True,
     )[None]

time: 251 us -> 252 us (level)
  no operation moved by 1% of the time
where the time goes in v6:
time: 252 us
  blocking collectives  85.1 us (34%)
  waiting for transfers between devices  77.5 us (31%)
  matrix products  30.4 us (12%)
  local copies, waits for them, and re-layouts  26.1 us (10%)
  between operations  13.9 us (6%)
  starting transfers between devices  13.2 us (5%)
  other arithmetic  5.41 us (2%)
    all_to_all x1, blocking collectives, shards(): lax.all_to_all(jnp.concatenate([send_rows, send_grad], axis=1).astype(jnp...  85.1 us
    all_to_all x1, waiting for transfers between devices, shards(): lax.all_to_all(grad_rows.reshape(groups, capacity, features), 'expert', s...  35.1 us
    all_to_all x1, waiting for transfers between devices, shards(): lax.all_to_all(output.reshape(groups, capacity, features), 'expert', spli...  30.3 us
    all_gather x1, waiting for transfers between devices, shards(): all_w = lax.all_gather(stacked, ('dx', 'dy'), axis=0, tiled=True)  11.5 us
    all_to_all x1, starting transfers between devices, shards(): lax.all_to_all(output.reshape(groups, capacity, features), 'expert', spli...  8.79 us
    reshape x1, local copies, waits for them, and re-layouts, shards(): weight_rows = all_w[:, 2 * hidden_units:].reshape(n_dp * rows_dp, features)  6.61 us
    dot_general x1, matrix products, shards(): lax.dot_general(jnp.concatenate([grad_gate, grad_up], axis=1), w_both, co...  5.85 us
    dot_general x1, matrix products, shards(): both_pre = jnp.dot(x_rows, w_both, preferred_element_type=jnp.float32)  5.27 us
  transfers between devices with their start and end apart: 5, of which 3 were waited for; matrix products, arithmetic and copies ran while one was open for 13% of the time, Pallas kernels for 0%

profile of v6, /device:TPU:1, one launch (start us, length us, event | category | flops | bytes accessed | tf_op | source)
XLA Modules:
  0.0 251.6 jit_solution(9642032343310247057)
XLA Ops:
  7.2 1.1 reshape_squeeze.3
  8.4 1.7 pad_maximum_fusion.1
  10.1 0.8 copy.25
  11.2 0.6 reduce-window.6
  12.3 0.8 slice_bitcast_fusion
  13.1 0.7 multiply_add_fusion.1
  13.8 1.6 fusion.22
  15.4 1.6 fusion.7
  16.9 1.4 concatenate.16
  18.4 1.5 convolution_convert_fusion.1
  19.9 2.4 concatenate.15
  22.3 1.7 pad_maximum_fusion
  24.0 85.1 %all_to_all.19 = bf16[16,18,4096]{2,1,0:T(8,128)(2,1)} all-to-all(bf16[16,18,4096]{2,1,0:T(8,128)(2,1)S(1)} %pad_maximum_fusion), channel_id=1, replica_groups=mesh['dx'=4,'dy'=8,'expert'=16] {'expert'}, dimensions={0} | all-to-all | bytes 4718592 | tf_op jit(solution)/shard_map/all_to_all | solution.py:45
  109.1 4.3 %all_to_all.13 = bf16[288,4096]{1,0:T(8,128)(2,1)} reshape(bf16[16,18,4096]{2,1,0:T(8,128)(2,1)} %all_to_all.19) | data formatting | bytes 4718592 | tf_op jit(solution)/shard_map/all_to_all | solution.py:45
  113.5 11.5 %all-gather.2.cloned.1.call-done = bf16[2048,2304]{1,0:T(8,128)(2,1)} async-done(((bf16[64,2304]{1,0:T(8,128)(2,1)}), bf16[2048,2304]{1,0:T(8,128)(2,1)}) %all-gather.2.cloned.1.call-update) | async-done | bytes 9437200 | tf_op jit(solution)/shard_map/all_gather | solution.py:22
  124.9 3.7 %slice.55 = bf16[2048,768]{1,0:T(8,128)(2,1)} slice(bf16[2048,2304]{1,0:T(8,128)(2,1)} %all-gather.2.cloned.1.call-done), slice={[0:2048], [1536:2304]} | slice | bytes 6291456 | tf_op jit(solution)/shard_map/slice | solution.py:24
  128.7 6.6 %reshape.93 = bf16[768,2048]{1,0:T(8,128)(2,1)} reshape(bf16[2048,768]{1,0:T(8,128)(2,1)} %slice.55) | data formatting | bytes 6291456 | tf_op jit(solution)/shard_map/reshape | solution.py:24
  135.3 5.3 %fusion.2 = f32[288,1536]{1,0:T(8,128)S(1)} fusion(bf16[2048,2304]{1,0:T(8,128)(2,1)} %all-gather.2.cloned.1.call-done, bf16[288,4096]{1,0:T(8,128)(2,1)} %all_to_all.13), kind=kOutput, calls=%fused_computation.2 | convolution fusion | flops 1811939328 | bytes 9240576 | tf_op jit(solution)/shard_map/dot_general | solution.py:54
  140.6 2.2 multiply_convert_fusion.1
  143.1 4.7 %convolution_convert_fusion = bf16[768,2048]{1,0:T(8,128)(2,1)} fusion(bf16[288,768]{0,1:T(8,128)(2,1)S(1)} %bitcast.53, bf16[288,4096]{1,0:T(8,128)(2,1)} %all_to_all.13), kind=kOutput, calls=%fused_computation.4 | convolution fusion | flops 907542528 | bytes 4767744 | tf_op jit(solution)/shard_map/dot_general | solution.py:68
  147.8 3.0 %convolution_convert_fusion.2 = bf16[288,2048]{1,0:T(8,128)(2,1)S(1)} fusion(bf16[288,768]{1,0:T(8,128)(2,1)S(1)} %get-tuple-element.9, bf16[768,2048]{1,0:T(8,128)(2,1)} %reshape.93), kind=kOutput, calls=%fused_computation.10 | convolution fusion | flops 906559488 | bytes 4767744 | tf_op jit(solution)/shard_map/dot_general | solution.py:71
  150.8 1.4 reshape.94
  152.2 8.8 %all-to-all-start.1 = ((bf16[16,18,2048]{2,1,0:T(8,128)(2,1)}), bf16[16,18,2048]{2,1,0:T(8,128)(2,1)S(1)}, u32[]{:S(2)}, u32[]{:S(2)}) async-start(bf16[16,18,2048]{2,1,0:T(8,128)(2,1)} %reshape.94), calls=%async_computation.1 | async-start | bytes 3145728 | tf_op jit(solution)/shard_map/all_to_all | solution.py:72
  161.0 5.8 %fusion.4 = bf16[288,2048]{1,0:T(8,128)(2,1)} fusion(bf16[2048,2304]{1,0:T(8,128)(2,1)} %all-gather.2.cloned.1.call-done, bf16[288,768]{1,0:T(8,128)(2,1)S(1)} %copy-done.4, bf16[288,768]{1,0:T(8,128)(2,1)S(1)} %get-tuple-element.6), kind=kOutput, calls=%fused_computation.7 | convolution fusion | flops 1814298624 | bytes 8355840 | tf_op jit(solution)/shard_map/dot_general | solution.py:80
  166.8 2.4 reshape.95
  169.2 30.3 %all-to-all-done.1 = bf16[16,18,2048]{2,1,0:T(8,128)(2,1)S(1)} async-done(((bf16[16,18,2048]{2,1,0:T(8,128)(2,1)}), bf16[16,18,2048]{2,1,0:T(8,128)(2,1)S(1)}, u32[]{:S(2)}, u32[]{:S(2)}) %all-to-all-start.1) | async-done | bytes 1179680 | tf_op jit(solution)/shard_map/all_to_all | solution.py:72
  199.5 4.3 %all-to-all-start.2 = ((bf16[16,18,2048]{2,1,0:T(8,128)(2,1)}), bf16[16,18,2048]{2,1,0:T(8,128)(2,1)}, u32[]{:S(2)}, u32[]{:S(2)}) async-start(bf16[16,18,2048]{2,1,0:T(8,128)(2,1)} %reshape.95), calls=%async_computation.2 | async-start | bytes 3145728 | tf_op jit(solution)/shard_map/all_to_all | solution.py:86
  203.9 0.6 reduce-scatter.5.cloned.1.call-update
  205.1 1.5 fusion.12
  206.6 0.6 pad_maximum_fusion.2
  207.2 35.1 %all-to-all-done.2 = bf16[16,18,2048]{2,1,0:T(8,128)(2,1)} async-done(((bf16[16,18,2048]{2,1,0:T(8,128)(2,1)}), bf16[16,18,2048]{2,1,0:T(8,128)(2,1)}, u32[]{:S(2)}, u32[]{:S(2)}) %all-to-all-start.2) | async-done | bytes 1179680 | tf_op jit(solution)/shard_map/all_to_all | solution.py:86
  242.3 2.8 %fusion.8 = bf16[128,2048]{1,0:T(8,128)(2,1)} fusion(bf16[16,18,2048]{2,1,0:T(8,128)(2,1)} %all-to-all-done.2, s32[128]{0:T(128)S(1)} %get-tuple-element.10, s32[16,18]{1,0:T(8,128)S(1)} %multiply_add_fusion, s32[128]{0:T(128)S(1)} %get-tuple-element.11), kind=kOutput, calls=%fused_computation.14 | convolution fusion | flops 151441408 | bytes 1706112 | tf_op jit(solution)/shard_map/dot_general | solution.py:102
  (31 shorter events, 1.9 us)
Async XLA Ops:
  7.2 11.2 %copy-start = (bf16[128,2048]{1,0:T(8,128)(2,1)S(1)}, bf16[128,2048]{1,0:T(8,128)(2,1)}, u32[]{:S(2)}) copy-start(bf16[128,2048]{1,0:T(8,128)(2,1)} %param.7) | copy-start | bytes 1572868
  7.2 8.2 %copy-start.1 = (bf16[128,2048]{1,0:T(8,128)(2,1)S(1)}, bf16[128,2048]{1,0:T(8,128)(2,1)}, u32[]{:S(2)}) copy-start(bf16[128,2048]{1,0:T(8,128)(2,1)} %param.8) | copy-start | bytes 1572868
  7.2 117.7 %all-gather.2.cloned.1.call-start = ((), (), s32[]{:S(2)}) async-start(), calls=%async_computation.5 | async-start | bytes 9732096 | tf_op jit(solution)/shard_map/all_gather | solution.py:22
  10.1 193.8 %reduce-scatter.3.cloned.1.call-start = ((), (), s32[]{:S(2)}) async-start(), calls=%async_computation.6 | async-start | bytes 3538944 | tf_op jit(solution)/shard_map/reduce_scatter | solution.py:106
  135.3 5.3 %copy-start.2 = (bf16[768,2048]{1,0:T(8,128)(2,1)S(1)}, bf16[768,2048]{1,0:T(8,128)(2,1)}, u32[]{:S(2)}) copy-start(bf16[768,2048]{1,0:T(8,128)(2,1)} %reshape.93) | copy-start | bytes 9437188
  135.3 5.3 %copy-start.3 = (bf16[288,4096]{1,0:T(8,128)(2,1)S(1)}, bf16[288,4096]{1,0:T(8,128)(2,1)}, u32[]{:S(2)}) copy-start(bf16[288,4096]{1,0:T(8,128)(2,1)} %all_to_all.13) | copy-start | bytes 7077892
  150.8 10.2 %copy-start.4 = (bf16[288,768]{1,0:T(8,128)(2,1)S(1)}, bf16[288,768]{1,0:T(8,128)(2,1)}, u32[]{:S(2)}) copy-start(bf16[288,768]{1,0:T(8,128)(2,1)} %get-tuple-element.7) | copy-start | bytes 1327108
  152.2 47.3 %all-to-all-start.1 = ((bf16[16,18,2048]{2,1,0:T(8,128)(2,1)}), bf16[16,18,2048]{2,1,0:T(8,128)(2,1)S(1)}, u32[]{:S(2)}, u32[]{:S(2)}) async-start(bf16[16,18,2048]{2,1,0:T(8,128)(2,1)} %reshape.94), calls=%async_computation.1 | async-start | bytes 3145728 | tf_op jit(solution)/shard_map/all_to_all | solution.py:72
  199.5 42.8 %all-to-all-start.2 = ((bf16[16,18,2048]{2,1,0:T(8,128)(2,1)}), bf16[16,18,2048]{2,1,0:T(8,128)(2,1)}, u32[]{:S(2)}, u32[]{:S(2)}) async-start(bf16[16,18,2048]{2,1,0:T(8,128)(2,1)} %reshape.95), calls=%async_computation.2 | async-start | bytes 3145728 | tf_op jit(solution)/shard_map/all_to_all | solution.py:86
  203.8 41.2 %reduce-scatter.5.cloned.1.call-start = ((), (), s32[]{:S(2)}) async-start(), calls=%async_computation.7 | async-start | bytes 491520 | tf_op jit(solution)/shard_map/reduce_scatter | solution.py:105
Sparse Core Ops, SparseCore 0:
  11.7 113.1 all-gather.1
  147.9 44.4 reduce-scatter.2
  208.0 21.4 reduce-scatter.4
